TPU v7x, 128 devices: a whole 4x4x4 slice. The times are simulated.
128 devices in a mesh: shard: 8 (over y, core), tensor: 4 (over z), section: 4 (over x).
Axes of the slice: x: 4, y: 4, z: 4, core: 2. Of those that a mesh axis runs over, the one named last changes fastest.
Arguments:
- activations: bfloat16 [4, 16384, 2048], P('section', 'shard'), may hold values from -500 to 500, as said below
- out_grad: bfloat16 [4, 16384, 8192], P('section', 'shard', 'tensor'), may hold values from -30 to 30, as said below
- basis: float32 [4, 2048, 256], P('section', 'shard'), may hold values from -0.125 to 0.125
- first_moment: float32 [4, 256, 8192], P('section', 'shard', 'tensor'), may hold values from -6 to 6
- second_moment: float32 [4, 256, 8192], P('section', 'shard', 'tensor'), may hold values from 0.5 to 2
- gain_partial: float32 [4, 8, 2048], P('section', 'shard'), may hold values from -4096 to 4096
- gain_first: float32 [4, 2048], P('section', 'shard'), may hold values from -6 to 6
- gain_second: float32 [4, 2048], P('section', 'shard'), may hold values from 0.5 to 2
Outputs:
- update: float32 [4, 2048, 8192], P('section', 'shard', 'tensor')
- first_out: float32 [4, 256, 8192], P('section', 'shard', 'tensor')
- second_out: float32 [4, 256, 8192], P('section', 'shard', 'tensor')
- new_basis: float32 [4, 2048, 256], P('section', ('shard', 'tensor'))
- gain_step: float32 [4, 2048], P('section', 'shard')
- gain_first_out: float32 [4, 2048], P('section', 'shard')
- gain_second_out: float32 [4, 2048], P('section', 'shard')
Inputs may be any that keep to these rules, and one draw needn't show every extreme that they name: Real-valued activations whose column scales differ from column to column. `out_grad`: Real-valued gradients whose column scales differ from column to column.
All inputs are finite; a program needn't handle non-finite values.
Results may differ from a plain program's by a relative error of at most 0.0003.
Values sent between devices are 32-bit elements; how exact they have to be, the bound alone decides.
No kernel may reach another device: no remote copies, remote signals or barrier semaphores. Data moves between devices by JAX's collectives and lax.ppermute only.
A program may use at most 128 MiB of HBM per device.

v0:
```python
import jax
import jax.numpy as jnp
from jax import lax
from jax.sharding import PartitionSpec as P

D = 2048
FF = 8192
NS_STEPS = 5
STEP = 8


exact_mode = lax.Precision.HIGHEST
beta_one = 0.9
beta_two = 0.999
adam_eps = 1e-08
clip_eps = 1e-06
ns_eps = 1e-07
coef_first = 3.4445
coef_second = -4.775
coef_third = 2.0315
PAD = 8
SHARD = ("chip_y", "core")


def adam_direction(clipped, first_old, second_old):
    first_new = beta_one * first_old + (1.0 - beta_one) * clipped
    second_new = beta_two * second_old + (1.0 - beta_two) * clipped * clipped
    direction = (
        first_new
        / (1.0 - beta_one**STEP)
        / (jnp.sqrt(second_new / (1.0 - beta_two**STEP)) + adam_eps)
    )
    return (first_new, second_new, direction)


ns_mode = lax.Precision.HIGH


def mixer_of(current):
    gram = jnp.dot(current.T, current, precision=ns_mode)
    return coef_second * gram + coef_third * jnp.dot(gram, gram, precision=ns_mode)


def split3(x):
    hi = lax.reduce_precision(x, exponent_bits=8, mantissa_bits=7)
    rest = x - hi
    mid = lax.reduce_precision(rest, exponent_bits=8, mantissa_bits=7)
    lo = rest - mid
    return tuple(p.astype(jnp.bfloat16) for p in (hi, mid, lo))


def dot_split(lhs, rhs_pieces, dims):
    out = None
    for piece in rhs_pieces:
        term = lax.dot_general(lhs, piece, dims, preferred_element_type=jnp.float32)
        out = term if out is None else out + term
    return out


def butterfly_sum(x, axis):
    n = lax.axis_size(axis)
    k = 1
    while k < n:
        x = x + lax.ppermute(x, axis, [(i, i ^ k) for i in range(n)])
        k *= 2
    return x


def chip_then_y_sum(x):
    core = lax.axis_index("core")
    half = x.shape[0] // 2
    swap = [(0, 1), (1, 0)]
    mine = lax.dynamic_slice_in_dim(x, core * half, half, 0)
    theirs = lax.dynamic_slice_in_dim(x, (1 - core) * half, half, 0)
    mine = mine + lax.ppermute(theirs, "core", swap)
    mine = lax.psum(mine, "chip_y")
    other = lax.ppermute(mine, "core", swap)
    first = jnp.where(core == 0, mine, other)
    second = jnp.where(core == 0, other, mine)
    return jnp.concatenate([first, second], axis=0)


def shards(
    activations, out_grad, basis, first_moment, second_moment, gain_partial, gain_first, gain_second
):
    tensors = lax.axis_size("tensor")
    shard_count = lax.axis_size(SHARD)
    shard_pos = lax.axis_index(SHARD)
    tensor_pos = lax.axis_index("tensor")
    layer_count = activations.shape[0]
    rows_here = basis.shape[1]
    rank_rows = first_moment.shape[1]
    cols_here = out_grad.shape[2]
    rank = basis.shape[2]
    out_rows = rows_here // tensors
    layer_index = 0
    tokens_in = activations[layer_index]
    grads_out = out_grad[layer_index]
    basis_here = basis[layer_index]

    partial_grad = lax.dot_general(
        tokens_in, grads_out, (((0,), (0,)), ((), ())), preferred_element_type=jnp.float32
    )
    grad_block = lax.psum_scatter(partial_grad, SHARD, scatter_dimension=0, tiled=True)
    part_proj = jnp.dot(basis_here.T, grad_block, precision=exact_mode)
    gain_row = gain_partial[layer_index, 0]
    gain_len = gain_row.shape[0]
    gain_rows = -(-gain_len // cols_here)
    gain_block = jnp.pad(gain_row, (0, gain_rows * cols_here - gain_len)).reshape(gain_rows, cols_here)
    square_part = jnp.sum(grad_block * grad_block)
    extra = jnp.zeros((2 * PAD - gain_rows % (2 * PAD), cols_here), jnp.float32).at[0, 0].set(square_part)
    packed = chip_then_y_sum(jnp.concatenate([part_proj, gain_block, extra], axis=0))
    proj_full = packed[:rank]
    square_shard = packed[rank + gain_rows, 0]
    gain_total = packed[rank:rank + gain_rows].reshape(-1)[:gain_len]
    proj_rows = lax.dynamic_slice_in_dim(proj_full, shard_pos * rank_rows, rank_rows, 0)

    refresh_part = lax.dot_general(
        grad_block, proj_full, (((1,), (1,)), ((), ())), precision=exact_mode
    )
    extra_r = jnp.zeros((PAD, rank), jnp.float32).at[0, 0].set(square_shard)
    packed_r = butterfly_sum(jnp.concatenate([refresh_part, extra_r], axis=0), "tensor")
    square_st = packed_r[rows_here, 0]
    refreshed = lax.all_gather(packed_r[:rows_here], SHARD, axis=0, tiled=True)

    gain_own = lax.dynamic_slice_in_dim(gain_total, shard_pos * rows_here, rows_here, 0)
    square_local = square_st + jnp.sum(gain_total * gain_total)
    total_sq = butterfly_sum(jnp.full((PAD, 128), square_local, jnp.float32), "section")[0, 0]
    entry_count = float(lax.axis_size("section") * layer_count * (D * FF + D))
    clip = jnp.minimum(1.0, lax.rsqrt(total_sq / entry_count + clip_eps))

    first_new, second_new, direction = adam_direction(
        clip * proj_rows, first_moment[layer_index], second_moment[layer_index]
    )
    update_here = jnp.dot(
        basis_here, lax.all_gather(direction, SHARD, axis=0, tiled=True), precision=exact_mode
    )

    current = refreshed / jnp.sqrt(jnp.sum(refreshed * refreshed) + ns_eps)
    for step_index in range(NS_STEPS - 1):
        current = coef_first * current + jnp.dot(current, mixer_of(current), precision=ns_mode)
    row_start = shard_pos * rows_here + tensor_pos * out_rows
    own = lax.dynamic_slice_in_dim(current, row_start, out_rows, 0)
    own = coef_first * own + jnp.dot(own, mixer_of(current), precision=ns_mode)

    gain_first_new, gain_second_new, gain_dir = adam_direction(
        clip * gain_own, gain_first[layer_index], gain_second[layer_index]
    )
    return (
        update_here[None],
        first_new[None],
        second_new[None],
        own[None],
        gain_dir[None],
        gain_first_new[None],
        gain_second_new[None],
    )


def solution(mesh):
    names = mesh.axis_names
    sizes = dict(mesh.shape)
    chip_y = sizes["shard"] // 2
    split_shape = []
    split_names = []
    for name in names:
        if name == "shard":
            split_shape += [chip_y, 2]
            split_names += ["chip_y", "core"]
        else:
            split_shape.append(sizes[name])
            split_names.append(name)
    split = jax.sharding.Mesh(mesh.devices.reshape(split_shape), tuple(split_names))
    placed = (
        P("section", SHARD, None),
        P("section", SHARD, "tensor"),
        P("section", SHARD, None),
        P("section", SHARD, "tensor"),
        P("section", SHARD, "tensor"),
        P("section", SHARD, None),
        P("section", SHARD),
        P("section", SHARD),
    )
    return jax.shard_map(
        shards,
        mesh=split,
        in_specs=placed,
        out_specs=(
            P("section", SHARD, "tensor"),
            P("section", SHARD, "tensor"),
            P("section", SHARD, "tensor"),
            P("section", SHARD + ("tensor",), None),
            P("section", SHARD),
            P("section", SHARD),
            P("section", SHARD),
        ),
        check_vma=False,
    )
```

profile of v0, /device:TPU:1, one launch (start us, length us, event | category | flops | bytes accessed | tf_op | source)
XLA Modules:
  0.0 281.3 jit_solution(16113410873973965776)
XLA Ops:
  7.2 0.0 copy-start
  7.2 0.0 reduce-scatter.2.cloned.1.call-start
  7.2 24.3 %fusion = f32[2048,2048]{1,0:T(8,128)} fusion(bf16[1,2048,2048]{2,1,0:T(8,128)(2,1)} %param.13, bf16[1,2048,2048]{2,1,0:T(8,128)(2,1)} %param.12), kind=kOutput, calls=%fused_computation | convolution fusion | flops 17179869184 | bytes 33554432 | tf_op jit(solution)/shard_map/dot_general | solution.py:101
  31.6 0.0 reduce-scatter.2.cloned.1.call-update
  31.6 0.0 all-reduce.4.cloned.1.call-start
  31.6 94.5 %reduce-scatter.2.cloned.1.call-done = f32[256,2048]{1,0:T(8,128)} async-done(((f32[2048,2048]{1,0:T(8,128)}), f32[256,2048]{1,0:T(8,128)}) %reduce-scatter.2.cloned.1.call-update) | async-done | bytes 2097168 | tf_op jit(solution)/shard_map/reduce_scatter | solution.py:104
  126.2 2.9 %multiply_reduce_fusion.1 = f32[]{:T(128)} fusion(f32[256,2048]{1,0:T(8,128)} %reduce-scatter.2.cloned.1.call-done), kind=kLoop, calls=%fused_computation.16 | loop fusion | flops 1048575 | bytes 2097156 | tf_op jit(solution)/shard_map/reduce_sum | solution.py:110
  129.1 2.0 convolution_bitcast_fusion.1
  131.1 0.9 select_maximum_fusion
  132.0 1.4 copy-done.4
  133.4 0.1 constant_dynamic-slice_fusion.1
  133.5 1.3 collective-permute-start
  134.8 2.5 collective-permute-done
  137.3 2.7 dynamic-slice_add_fusion
  140.0 0.0 all-reduce.4.cloned.1.call-update
  140.0 0.0 all-gather.5.cloned.1.call-start
  140.1 44.4 %all-reduce.4.cloned.1.call-done = f32[136,2048]{1,0:T(8,128)} async-done(((f32[136,2048]{1,0:T(8,128)}), f32[136,2048]{1,0:T(8,128)}) %all-reduce.4.cloned.1.call-update) | async-done | bytes 1114128 | tf_op jit(solution)/shard_map/psum | solution.py:76
  184.5 2.1 collective-permute-start.1
  186.6 2.7 collective-permute-done.1
  189.3 1.7 broadcast_select_fusion.1
  191.0 0.0 copy-start.2
  191.0 0.5 slice.56
  191.6 1.9 fusion.3
  193.5 0.0 copy-start.6
  193.5 0.7 select_maximum_fusion.1
  194.2 1.4 collective-permute-start.2
  195.6 6.4 %collective-permute-done.2 = f32[264,256]{1,0:T(8,128)S(1)} collective-permute-done((f32[264,256]{1,0:T(8,128)S(1)}, f32[264,256]{1,0:T(8,128)S(1)}, u32[]{:S(2)}, u32[]{:S(2)}) %collective-permute-start.2) | collective-permute-done | bytes 270368 | tf_op jit(solution)/shard_map/ppermute | solution.py:64
  202.0 0.7 fusion.25
  202.6 2.9 %collective-permute-start.3 = (f32[264,256]{1,0:T(8,128)S(1)}, f32[264,256]{1,0:T(8,128)S(1)}, u32[]{:S(2)}, u32[]{:S(2)}) collective-permute-start(f32[264,256]{1,0:T(8,128)S(1)} %fusion.25), channel_id=1, source_target_pairs={{0,8},{4,12},{8,0},{12,4},{1,9},{5,13},{9,1},{13,5},{2,10},{6,14},... | collective-permute-start | bytes 811016 | tf_op jit(solution)/shard_map/ppermute | solution.py:64
  205.6 5.5 %collective-permute-done.3 = f32[264,256]{1,0:T(8,128)S(1)} collective-permute-done((f32[264,256]{1,0:T(8,128)S(1)}, f32[264,256]{1,0:T(8,128)S(1)}, u32[]{:S(2)}, u32[]{:S(2)}) %collective-permute-start.3) | collective-permute-done | bytes 270368 | tf_op jit(solution)/shard_map/ppermute | solution.py:64
  211.1 0.7 slice.59
  211.8 0.0 all-gather.5.cloned.1.call-update
  211.8 0.0 all-gather.3.cloned.1.call-start
  211.9 0.6 fusion.30
  212.5 0.5 slice.57
  214.3 1.3 collective-permute-start.4
  215.6 1.3 collective-permute-done.4
  216.9 2.7 collective-permute-start.5
  219.6 1.3 collective-permute-done.5
  220.8 0.5 slice.54
  222.1 0.8 fusion.17
  222.9 0.9 fusion.16
  223.8 0.0 all-gather.3.cloned.1.call-update
  223.9 0.6 add_divide_fusion.1
  224.5 15.6 %all-gather.5.cloned.1.call-done = f32[2048,256]{1,0:T(8,128)} async-done(((f32[256,256]{1,0:T(8,128)}), f32[2048,256]{1,0:T(8,128)}) %all-gather.5.cloned.1.call-update) | async-done | bytes 2097168 | tf_op jit(solution)/shard_map/all_gather | solution.py:124
  240.0 2.9 %multiply_reduce_fusion = f32[]{:T(128)} fusion(f32[2048,256]{1,0:T(8,128)} %all-gather.5.cloned.1.call-done), kind=kLoop, calls=%fused_computation.15 | loop fusion | flops 1048575 | bytes 2097156 | tf_op jit(solution)/shard_map/reduce_sum | solution.py:139
  243.6 1.8 fusion.27
  245.4 0.3 fusion.8
  245.7 1.0 fusion.26
  246.7 2.0 fusion.10
  248.8 0.3 fusion.7
  249.0 1.2 convolution_add_fusion.2
  250.3 1.9 fusion.31
  252.1 0.3 fusion.6
  252.4 1.1 convolution_add_fusion.1
  253.5 1.9 fusion.32
  255.6 0.3 fusion.5
  255.9 1.0 convolution_add_fusion
  256.9 1.9 fusion.33
  258.8 0.3 fusion.4
  259.1 0.8 fusion.9
  259.9 8.0 %all-gather.3.cloned.1.call-done = f32[256,2048]{1,0:T(8,128)} async-done(((f32[32,2048]{1,0:T(8,128)}), f32[256,2048]{1,0:T(8,128)}) %all-gather.3.cloned.1.call-update) | async-done | bytes 2097168 | tf_op jit(solution)/shard_map/all_gather | solution.py:136
  267.9 5.0 %convolution_bitcast_fusion = f32[1,256,2048]{1,2,0:T(8,128)S(1)} fusion(f32[256,2048]{1,0:T(8,128)} %all-gather.3.cloned.1.call-done, f32[1,256,256]{2,1,0:T(8,128)S(1)} %copy-done), kind=kOutput, calls=%fused_computation.6 | convolution fusion | flops 1610612736 | bytes 4456448 | tf_op jit(solution)/shard_map/dot_general | solution.py:135
  272.9 1.8 copy.15
  (22 shorter events, 0.1 us)
Async XLA Ops:
  7.2 121.9 %copy-start = (f32[1,256,256]{2,1,0:T(8,128)S(1)}, f32[1,256,256]{2,1,0:T(8,128)}, u32[]{:S(2)}) copy-start(f32[1,256,256]{2,1,0:T(8,128)} %param.14) | copy-start | bytes 786436
  7.2 119.0 %reduce-scatter.2.cloned.1.call-start = ((), (), s32[]{:S(2)}) async-start(), calls=%async_computation.1 | async-start | bytes 18874368 | tf_op jit(solution)/shard_map/reduce_scatter | solution.py:104
  31.6 152.9 %all-reduce.4.cloned.1.call-start = ((), (), s32[]{:S(2)}) async-start(), calls=%async_computation.2 | async-start | bytes 2228224 | tf_op jit(solution)/shard_map/psum | solution.py:76
  126.2 2.9 %copy-start.1 = (f32[256,2048]{1,0:T(8,128)S(1)}, f32[256,2048]{1,0:T(8,128)}, u32[]{:S(2)}) copy-start(f32[256,2048]{1,0:T(8,128)} %reduce-scatter.2.cloned.1.call-done) | copy-start | bytes 6291460
  129.1 2.0 copy-start.8
  132.0 1.4 copy-start.4
  133.5 3.8 %collective-permute-start = (f32[136,2048]{1,0:T(8,128)S(1)}, f32[136,2048]{1,0:T(8,128)}, u32[]{:S(2)}, u32[]{:S(2)}) collective-permute-start(f32[136,2048]{1,0:T(8,128)S(1)} %constant_dynamic-slice_fusion.1), channel_id=1, source_target_pairs={{0,16},{16,0},{1,17},{17,1},{2,18},{18,2},{3,19},{19,3},{4,20},{20... | collective-permute-start | bytes 3342344 | tf_op jit(solution)/shard_map/ppermute | solution.py:75
  140.0 100.0 %all-gather.5.cloned.1.call-start = ((), (), s32[]{:S(2)}) async-start(), calls=%async_computation.4 | async-start | bytes 2359296 | tf_op jit(solution)/shard_map/all_gather | solution.py:124
  184.5 4.8 %collective-permute-start.1 = (f32[136,2048]{1,0:T(8,128)}, f32[136,2048]{1,0:T(8,128)}, u32[]{:S(2)}, u32[]{:S(2)}) collective-permute-start(f32[136,2048]{1,0:T(8,128)} %all-reduce.4.cloned.1.call-done), channel_id=1, source_target_pairs={{0,16},{16,0},{1,17},{17,1},{2,18},{18,2},{3,19},{19,3},{4,20},{20... | collective-permute-start | bytes 3342344 | tf_op jit(solution)/shard_map/ppermute | solution.py:77
  191.0 2.5 copy-start.2
  193.5 28.6 %copy-start.6 = (f32[1,32,2048]{2,1,0:T(8,128)S(1)}, f32[1,32,2048]{2,1,0:T(8,128)}, u32[]{:S(2)}) copy-start(f32[1,32,2048]{2,1,0:T(8,128)} %param.16) | copy-start | bytes 786436
  194.2 27.9 %copy-start.3 = (f32[136,2048]{1,0:T(8,128)S(1)}, f32[136,2048]{1,0:T(8,128)}, u32[]{:S(2)}) copy-start(f32[136,2048]{1,0:T(8,128)} %copy-done.2) | copy-start | bytes 3342340
  194.2 7.7 %collective-permute-start.2 = (f32[264,256]{1,0:T(8,128)S(1)}, f32[264,256]{1,0:T(8,128)S(1)}, u32[]{:S(2)}, u32[]{:S(2)}) collective-permute-start(f32[264,256]{1,0:T(8,128)S(1)} %select_maximum_fusion.1), channel_id=1, source_target_pairs={{0,4},{4,0},{8,12},{12,8},{1,5},{5,1},{9,13},{13,9},{2,6},{6,2},{1... | collective-permute-start | bytes 811016 | tf_op jit(solution)/shard_map/ppermute | solution.py:64
  202.6 8.4 %collective-permute-start.3 = (f32[264,256]{1,0:T(8,128)S(1)}, f32[264,256]{1,0:T(8,128)S(1)}, u32[]{:S(2)}, u32[]{:S(2)}) collective-permute-start(f32[264,256]{1,0:T(8,128)S(1)} %fusion.25), channel_id=1, source_target_pairs={{0,8},{4,12},{8,0},{12,4},{1,9},{5,13},{9,1},{13,5},{2,10},{6,14},... | collective-permute-start | bytes 811016 | tf_op jit(solution)/shard_map/ppermute | solution.py:64
  211.1 11.8 %copy-start.7 = (f32[1,32,2048]{2,1,0:T(8,128)S(1)}, f32[1,32,2048]{2,1,0:T(8,128)}, u32[]{:S(2)}) copy-start(f32[1,32,2048]{2,1,0:T(8,128)} %param.15) | copy-start | bytes 786436
  211.8 56.0 %all-gather.3.cloned.1.call-start = ((), (), s32[]{:S(2)}) async-start(), calls=%async_computation.3 | async-start | bytes 2359296 | tf_op jit(solution)/shard_map/all_gather | solution.py:136
  214.3 2.5 collective-permute-start.4
  216.9 4.0 %collective-permute-start.5 = (f32[8,128]{1,0:T(8,128)S(1)}, f32[8,128]{1,0:T(8,128)S(1)}, u32[]{:S(2)}, u32[]{:S(2)}) collective-permute-start(f32[8,128]{1,0:T(8,128)S(1)} %broadcast_add_fusion), channel_id=1, source_target_pairs={{0,2},{1,3},{2,0},{3,1},{4,6},{5,7},{6,4},{7,5},{8,10},{9,11},{10,... | collective-permute-start | bytes 12296 | tf_op jit(solution)/shard_map/ppermute | solution.py:64
  222.1 1.8 copy-start.9
  222.1 1.8 copy-start.10
  240.0 3.6 %copy-start.5 = (f32[2048,256]{1,0:T(8,128)S(1)}, f32[2048,256]{1,0:T(8,128)}, u32[]{:S(2)}) copy-start(f32[2048,256]{1,0:T(8,128)} %all-gather.5.cloned.1.call-done) | copy-start | bytes 6291460
Sparse Core Ops, SparseCore 0:
  31.7 94.4 reduce-scatter.1
  140.2 44.2 all-reduce.3
  212.0 28.0 all-gather.4
  242.2 25.6 all-gather.2
where the time goes:
time: 282 us; the launch traced here: 281 us
  waiting for transfers between devices  182 us (65%)
  matrix products  49.3 us (17%)
  between operations  17 us (6%)
  other arithmetic  15.5 us (5%)
  starting transfers between devices  11.8 us (4%)
  local copies, waits for them, and re-layouts  5.64 us (2%)
    reduce_scatter x1, waiting for transfers between devices, shards(): lax.psum_scatter(partial_grad, SHARD, scatter_dimension=0, tiled=True)  94.5 us
    psum x1, waiting for transfers between devices, chip_then_y_sum(): mine = lax.psum(mine, 'chip_y')  44.4 us
    dot_general x1, matrix products, shards(): lax.dot_general(tokens_in, grads_out, (((0,), (0,)), ((), ())), preferred...  24.3 us
    all_gather x1, waiting for transfers between devices, shards(): refreshed = lax.all_gather(packed_r[:rows_here], SHARD, axis=0, tiled=True)  15.6 us
    ppermute x4, waiting for transfers between devices, butterfly_sum(): x = x + lax.ppermute(x, axis, [(i, i ^ k) for i in range(n)])  14.4 us
    dot_general x5, matrix products, mixer_of(): gram = jnp.dot(current.T, current, precision=ns_mode)  9.45 us
    ppermute x4, starting transfers between devices, butterfly_sum(): x = x + lax.ppermute(x, axis, [(i, i ^ k) for i in range(n)])  8.25 us
    all_gather x1, waiting for transfers between devices, shards(): lax.all_gather(direction, SHARD, axis=0, tiled=True)  7.96 us
  transfers between devices with their start and end apart: 10, of which 10 were waited for; matrix products, arithmetic and copies ran while one was open for 8% of the time, Pallas kernels for 0%

commit v1 on v0

--- a/solution.py
+++ b/solution.py
@@ -78,6 +78,19 @@
     first = jnp.where(core == 0, mine, other)
     second = jnp.where(core == 0, other, mine)
     return jnp.concatenate([first, second], axis=0)
+
+
+def gather_doubling(x):
+    n = lax.axis_size(SHARD)
+    pos = lax.axis_index(SHARD)
+    buf = x
+    k = 1
+    while k < n:
+        other = lax.ppermute(buf, SHARD, [(i, i ^ k) for i in range(n)])
+        low = (pos // k) % 2 == 0
+        buf = jnp.where(low, jnp.concatenate([buf, other], 0), jnp.concatenate([other, buf], 0))
+        k *= 2
+    return buf
 
 
 def shards(
@@ -133,7 +146,7 @@
         clip * proj_rows, first_moment[layer_index], second_moment[layer_index]
     )
     update_here = jnp.dot(
-        basis_here, lax.all_gather(direction, SHARD, axis=0, tiled=True), precision=exact_mode
+        basis_here, gather_doubling(direction), precision=exact_mode
     )
 
     current = refreshed / jnp.sqrt(jnp.sum(refreshed * refreshed) + ns_eps)

time: 282 us -> 309 us (1.096)
  waiting for transfers between devices: 182 us -> 200 us
  starting transfers between devices: 11.8 us -> 19.3 us
    ppermute x0 -> x3, waiting for transfers between devices: none -> 43 us  [gather_doubling(): other = lax.ppermute(buf, SHARD, [(i, i ^ k) for i in range(n)])]
    all_gather x1, waiting for transfers between devices: 15.6 us -> 0.01 us  [shards(): refreshed = lax.all_gather(packed_r[:rows_here], SHARD, axis=0, tiled=True)]
    all_gather x1 -> x0, waiting for transfers between devices: 7.96 us -> none  [shards(): lax.all_gather(direction, SHARD, axis=0, tiled=True)]
    ppermute x0 -> x3, starting transfers between devices: none -> 7.61 us  [gather_doubling(): other = lax.ppermute(buf, SHARD, [(i, i ^ k) for i in range(n)])]
  transfers between devices with their start and end apart: 10 -> 12, of which waited for: 10 -> 11; matrix products, arithmetic and copies ran while one was open for 8% -> 4% of each run, Pallas kernels for 0% -> 0%
where the time goes in v1:
time: 309 us; the launch traced here: 307 us
  waiting for transfers between devices  200 us (65%)
  matrix products  49.5 us (16%)
  starting transfers between devices  19.3 us (6%)
  between operations  16.7 us (5%)
  other arithmetic  15.5 us (5%)
  local copies, waits for them, and re-layouts  5.62 us (2%)
    reduce_scatter x1, waiting for transfers between devices, shards(): lax.psum_scatter(partial_grad, SHARD, scatter_dimension=0, tiled=True)  94.5 us
    psum x1, waiting for transfers between devices, chip_then_y_sum(): mine = lax.psum(mine, 'chip_y')  44.4 us
    ppermute x3, waiting for transfers between devices, gather_doubling(): other = lax.ppermute(buf, SHARD, [(i, i ^ k) for i in range(n)])  43 us
    dot_general x1, matrix products, shards(): lax.dot_general(tokens_in, grads_out, (((0,), (0,)), ((), ())), preferred...  24.3 us
    ppermute x4, waiting for transfers between devices, butterfly_sum(): x = x + lax.ppermute(x, axis, [(i, i ^ k) for i in range(n)])  13 us
    dot_general x5, matrix products, mixer_of(): gram = jnp.dot(current.T, current, precision=ns_mode)  9.45 us
    ppermute x4, starting transfers between devices, butterfly_sum(): x = x + lax.ppermute(x, axis, [(i, i ^ k) for i in range(n)])  8.25 us
    ppermute x3, starting transfers between devices, gather_doubling(): other = lax.ppermute(buf, SHARD, [(i, i ^ k) for i in range(n)])  7.61 us
  transfers between devices with their start and end apart: 12, of which 11 were waited for; matrix products, arithmetic and copies ran while one was open for 4% of the time, Pallas kernels for 0%

profile of v1, /device:TPU:1, one launch (start us, length us, event | category | flops | bytes accessed | tf_op | source)
XLA Modules:
  0.0 307.0 jit_solution(13457721064136632831)
XLA Ops:
  7.2 0.0 reduce-scatter.2.cloned.1.call-start
  7.2 24.3 %fusion = f32[2048,2048]{1,0:T(8,128)} fusion(bf16[1,2048,2048]{2,1,0:T(8,128)(2,1)} %param.13, bf16[1,2048,2048]{2,1,0:T(8,128)(2,1)} %param.12), kind=kOutput, calls=%fused_computation | convolution fusion | flops 17179869184 | bytes 33554432 | tf_op jit(solution)/shard_map/dot_general | solution.py:114
  31.6 0.0 reduce-scatter.2.cloned.1.call-update
  31.6 0.0 all-reduce.4.cloned.1.call-start
  31.6 94.5 %reduce-scatter.2.cloned.1.call-done = f32[256,2048]{1,0:T(8,128)} async-done(((f32[2048,2048]{1,0:T(8,128)}), f32[256,2048]{1,0:T(8,128)}) %reduce-scatter.2.cloned.1.call-update) | async-done | bytes 2097168 | tf_op jit(solution)/shard_map/reduce_scatter | solution.py:117
  126.2 2.9 multiply_reduce_fusion.1
  129.1 2.0 convolution_bitcast_fusion.1
  131.1 0.9 select_maximum_fusion
  132.0 1.4 copy-done.4
  133.4 0.1 constant_dynamic-slice_fusion.1
  133.5 1.3 collective-permute-start
  134.8 2.5 collective-permute-done
  137.3 2.7 dynamic-slice_add_fusion
  140.0 0.0 all-reduce.4.cloned.1.call-update
  140.0 0.0 all-gather.2.cloned.1.call-start
  140.1 44.4 %all-reduce.4.cloned.1.call-done = f32[136,2048]{1,0:T(8,128)} async-done(((f32[136,2048]{1,0:T(8,128)}), f32[136,2048]{1,0:T(8,128)}) %all-reduce.4.cloned.1.call-update) | async-done | bytes 1114128 | tf_op jit(solution)/shard_map/psum | solution.py:76
  184.5 2.1 collective-permute-start.1
  186.6 2.7 collective-permute-done.1
  189.3 1.7 broadcast_select_fusion.1
  191.0 0.5 slice.56
  191.6 1.9 fusion.3
  193.5 0.7 select_maximum_fusion.1
  194.2 1.4 collective-permute-start.2
  195.6 6.4 %collective-permute-done.2 = f32[264,256]{1,0:T(8,128)S(1)} collective-permute-done((f32[264,256]{1,0:T(8,128)S(1)}, f32[264,256]{1,0:T(8,128)S(1)}, u32[]{:S(2)}, u32[]{:S(2)}) %collective-permute-start.2) | collective-permute-done | bytes 270368 | tf_op jit(solution)/shard_map/ppermute | solution.py:64
  202.0 0.7 fusion.32
  202.6 2.9 collective-permute-start.3
  205.6 0.6 fusion.37
  206.2 4.8 %collective-permute-done.3 = f32[264,256]{1,0:T(8,128)S(1)} collective-permute-done((f32[264,256]{1,0:T(8,128)S(1)}, f32[264,256]{1,0:T(8,128)S(1)}, u32[]{:S(2)}, u32[]{:S(2)}) %collective-permute-start.3) | collective-permute-done | bytes 270368 | tf_op jit(solution)/shard_map/ppermute | solution.py:64
  211.1 0.5 slice.57
  212.9 1.3 collective-permute-start.4
  214.2 1.3 collective-permute-done.4
  215.5 2.7 collective-permute-start.5
  218.2 0.7 slice.59
  218.9 0.0 all-gather.2.cloned.1.call-update
  218.9 0.5 collective-permute-done.5
  219.4 0.5 slice.54
  220.7 0.8 fusion.23
  221.4 0.9 fusion.22
  222.3 4.4 %collective-permute-start.6 = (f32[32,2048]{1,0:T(8,128)S(1)}, f32[32,2048]{1,0:T(8,128)S(1)}, u32[]{:S(2)}, u32[]{:S(2)}) collective-permute-start(f32[32,2048]{1,0:T(8,128)S(1)} %get-tuple-element.48), channel_id=1, source_target_pairs={{0,16},{16,0},{32,48},{48,32},{64,80},{80,64},{96,112},{112,96},{1... | collective-permute-start | bytes 786440 | tf_op jit(solution)/shard_map/ppermute | solution.py:89
  226.7 1.2 collective-permute-done.6
  227.9 0.8 collective-permute-start.7
  228.7 20.3 %collective-permute-done.7 = f32[64,2048]{1,0:T(8,128)S(1)} collective-permute-done((f32[64,2048]{1,0:T(8,128)S(1)}, f32[64,2048]{1,0:T(8,128)S(1)}, u32[]{:S(2)}, u32[]{:S(2)}) %collective-permute-start.7) | collective-permute-done | bytes 524320 | tf_op jit(solution)/shard_map/ppermute | solution.py:89
  249.0 0.1 maximum_select_fusion.2
  249.1 2.4 collective-permute-start.8
  251.6 0.6 add_divide_fusion.1
  252.2 21.5 %collective-permute-done.8 = f32[128,2048]{1,0:T(8,128)} collective-permute-done((f32[128,2048]{1,0:T(8,128)S(1)}, f32[128,2048]{1,0:T(8,128)}, u32[]{:S(2)}, u32[]{:S(2)}) %collective-permute-start.8) | collective-permute-done | bytes 1048608 | tf_op jit(solution)/shard_map/ppermute | solution.py:89
  273.7 5.0 %convolution_bitcast_fusion = f32[1,256,2048]{1,2,0:T(8,128)S(1)} fusion(f32[128,2048]{1,0:T(8,128)} %collective-permute-done.8, f32[128,2048]{1,0:T(8,128)S(1)} %maximum_select_fusion.2, pred[]{:T(512)S(6)} %eq.17, f32[1,256,256]{2,1,0:T(8,128)S(1)} %copy-done), kind=kOutput, calls=%fused_computation.6 | convolution fusion | flops 1612185600 | bytes 4456449 | tf_op jit(solution)/shard_map/dot_general | solution.py:148
  278.7 1.8 copy.15
  280.5 2.9 multiply_reduce_fusion
  284.1 1.8 fusion.34
  285.9 0.3 fusion.13
  286.2 1.0 fusion.33
  287.2 2.0 fusion.16
  289.2 0.3 fusion.12
  289.5 1.2 convolution_add_fusion.2
  290.7 1.9 fusion.38
  292.6 0.3 fusion.11
  292.9 1.0 convolution_add_fusion.1
  293.9 1.9 fusion.39
  295.8 0.3 fusion.10
  296.1 1.3 convolution_add_fusion
  297.4 1.9 fusion.40
  299.3 0.3 fusion.9
  299.6 0.8 fusion.14
  (27 shorter events, 0.1 us)
Async XLA Ops:
  7.2 121.9 %copy-start = (f32[1,256,256]{2,1,0:T(8,128)S(1)}, f32[1,256,256]{2,1,0:T(8,128)}, u32[]{:S(2)}) copy-start(f32[1,256,256]{2,1,0:T(8,128)} %param.14) | copy-start | bytes 786436
  7.2 119.0 %reduce-scatter.2.cloned.1.call-start = ((), (), s32[]{:S(2)}) async-start(), calls=%async_computation.1 | async-start | bytes 18874368 | tf_op jit(solution)/shard_map/reduce_scatter | solution.py:117
  31.6 152.9 %all-reduce.4.cloned.1.call-start = ((), (), s32[]{:S(2)}) async-start(), calls=%async_computation.2 | async-start | bytes 2228224 | tf_op jit(solution)/shard_map/psum | solution.py:76
  126.2 2.9 copy-start.1
  129.1 2.0 copy-start.8
  132.0 1.4 copy-start.4
  133.5 3.8 %collective-permute-start = (f32[136,2048]{1,0:T(8,128)S(1)}, f32[136,2048]{1,0:T(8,128)}, u32[]{:S(2)}, u32[]{:S(2)}) collective-permute-start(f32[136,2048]{1,0:T(8,128)S(1)} %constant_dynamic-slice_fusion.1), channel_id=1, source_target_pairs={{0,16},{16,0},{1,17},{17,1},{2,18},{18,2},{3,19},{19,3},{4,20},{20... | collective-permute-start | bytes 3342344 | tf_op jit(solution)/shard_map/ppermute | solution.py:75
  140.0 140.4 %all-gather.2.cloned.1.call-start = ((), (), s32[]{:S(2)}) async-start(), calls=%async_computation.3 | async-start | bytes 2359296 | tf_op jit(solution)/shard_map/all_gather | solution.py:137
  184.5 4.8 %collective-permute-start.1 = (f32[136,2048]{1,0:T(8,128)}, f32[136,2048]{1,0:T(8,128)}, u32[]{:S(2)}, u32[]{:S(2)}) collective-permute-start(f32[136,2048]{1,0:T(8,128)} %all-reduce.4.cloned.1.call-done), channel_id=1, source_target_pairs={{0,16},{16,0},{1,17},{17,1},{2,18},{18,2},{3,19},{19,3},{4,20},{20... | collective-permute-start | bytes 3342344 | tf_op jit(solution)/shard_map/ppermute | solution.py:77
  191.0 2.5 copy-start.2
  193.5 27.2 %copy-start.6 = (f32[1,32,2048]{2,1,0:T(8,128)S(1)}, f32[1,32,2048]{2,1,0:T(8,128)}, u32[]{:S(2)}) copy-start(f32[1,32,2048]{2,1,0:T(8,128)} %param.16) | copy-start | bytes 786436
  194.2 26.4 %copy-start.3 = (f32[136,2048]{1,0:T(8,128)S(1)}, f32[136,2048]{1,0:T(8,128)}, u32[]{:S(2)}) copy-start(f32[136,2048]{1,0:T(8,128)} %copy-done.2) | copy-start | bytes 3342340
  194.2 7.7 %collective-permute-start.2 = (f32[264,256]{1,0:T(8,128)S(1)}, f32[264,256]{1,0:T(8,128)S(1)}, u32[]{:S(2)}, u32[]{:S(2)}) collective-permute-start(f32[264,256]{1,0:T(8,128)S(1)} %select_maximum_fusion.1), channel_id=1, source_target_pairs={{0,4},{4,0},{8,12},{12,8},{1,5},{5,1},{9,13},{13,9},{2,6},{6,2},{1... | collective-permute-start | bytes 811016 | tf_op jit(solution)/shard_map/ppermute | solution.py:64
  202.6 8.4 %collective-permute-start.3 = (f32[264,256]{1,0:T(8,128)S(1)}, f32[264,256]{1,0:T(8,128)S(1)}, u32[]{:S(2)}, u32[]{:S(2)}) collective-permute-start(f32[264,256]{1,0:T(8,128)S(1)} %fusion.32), channel_id=1, source_target_pairs={{0,8},{4,12},{8,0},{12,4},{1,9},{5,13},{9,1},{13,5},{2,10},{6,14},... | collective-permute-start | bytes 811016 | tf_op jit(solution)/shard_map/ppermute | solution.py:64
  211.1 10.4 %copy-start.7 = (f32[1,32,2048]{2,1,0:T(8,128)S(1)}, f32[1,32,2048]{2,1,0:T(8,128)}, u32[]{:S(2)}) copy-start(f32[1,32,2048]{2,1,0:T(8,128)} %param.15) | copy-start | bytes 786436
  212.9 2.5 collective-permute-start.4
  215.5 4.0 %collective-permute-start.5 = (f32[8,128]{1,0:T(8,128)S(1)}, f32[8,128]{1,0:T(8,128)S(1)}, u32[]{:S(2)}, u32[]{:S(2)}) collective-permute-start(f32[8,128]{1,0:T(8,128)S(1)} %broadcast_add_fusion), channel_id=1, source_target_pairs={{0,2},{1,3},{2,0},{3,1},{4,6},{5,7},{6,4},{7,5},{8,10},{9,11},{10,... | collective-permute-start | bytes 12296 | tf_op jit(solution)/shard_map/ppermute | solution.py:64
  221.4 30.1 %copy-start.9 = (f32[1,256]{1,0:T(1,128)S(1)}, f32[1,256]{1,0:T(1,128)}, u32[]{:S(2)}) copy-start(f32[1,256]{1,0:T(1,128)} %param.18) | copy-start | bytes 3076
  221.4 30.1 %copy-start.10 = (f32[1,256]{1,0:T(1,128)S(1)}, f32[1,256]{1,0:T(1,128)}, u32[]{:S(2)}) copy-start(f32[1,256]{1,0:T(1,128)} %param.19) | copy-start | bytes 3076
  222.3 5.5 %collective-permute-start.6 = (f32[32,2048]{1,0:T(8,128)S(1)}, f32[32,2048]{1,0:T(8,128)S(1)}, u32[]{:S(2)}, u32[]{:S(2)}) collective-permute-start(f32[32,2048]{1,0:T(8,128)S(1)} %get-tuple-element.48), channel_id=1, source_target_pairs={{0,16},{16,0},{32,48},{48,32},{64,80},{80,64},{96,112},{112,96},{1... | collective-permute-start | bytes 786440 | tf_op jit(solution)/shard_map/ppermute | solution.py:89
  227.9 21.1 %collective-permute-start.7 = (f32[64,2048]{1,0:T(8,128)S(1)}, f32[64,2048]{1,0:T(8,128)S(1)}, u32[]{:S(2)}, u32[]{:S(2)}) collective-permute-start(f32[64,2048]{1,0:T(8,128)S(1)} %maximum_select_fusion.3), channel_id=1, source_target_pairs={{0,32},{16,48},{32,0},{48,16},{64,96},{80,112},{96,64},{112,80},{1... | collective-permute-start | bytes 1572872 | tf_op jit(solution)/shard_map/ppermute | solution.py:89
  249.1 24.5 %collective-permute-start.8 = (f32[128,2048]{1,0:T(8,128)S(1)}, f32[128,2048]{1,0:T(8,128)}, u32[]{:S(2)}, u32[]{:S(2)}) collective-permute-start(f32[128,2048]{1,0:T(8,128)S(1)} %maximum_select_fusion.2), channel_id=1, source_target_pairs={{0,64},{16,80},{32,96},{48,112},{64,0},{80,16},{96,32},{112,48},{1... | collective-permute-start | bytes 3145736 | tf_op jit(solution)/shard_map/ppermute | solution.py:89
  280.5 3.6 %copy-start.5 = (f32[2048,256]{1,0:T(8,128)S(1)}, f32[2048,256]{1,0:T(8,128)}, u32[]{:S(2)}) copy-start(f32[2048,256]{1,0:T(8,128)} %all-gather.2.cloned.1.call-done) | copy-start | bytes 6291460
Sparse Core Ops, SparseCore 0:
  31.7 94.4 reduce-scatter.1
  140.2 44.2 all-reduce.3
  219.0 32.6 all-gather.1

commit v2 on v0

--- a/solution.py
+++ b/solution.py
@@ -98,10 +98,14 @@
     grads_out = out_grad[layer_index]
     basis_here = basis[layer_index]
 
-    partial_grad = lax.dot_general(
-        tokens_in, grads_out, (((0,), (0,)), ((), ())), preferred_element_type=jnp.float32
-    )
-    grad_block = lax.psum_scatter(partial_grad, SHARD, scatter_dimension=0, tiled=True)
+    col_half = cols_here // 2
+    grad_halves = []
+    for piece in (grads_out[:, :col_half], grads_out[:, col_half:]):
+        partial_grad = lax.dot_general(
+            tokens_in, piece, (((0,), (0,)), ((), ())), preferred_element_type=jnp.float32
+        )
+        grad_halves.append(lax.psum_scatter(partial_grad, SHARD, scatter_dimension=0, tiled=True))
+    grad_block = jnp.concatenate(grad_halves, axis=1)
     part_proj = jnp.dot(basis_here.T, grad_block, precision=exact_mode)
     gain_row = gain_partial[layer_index, 0]
     gain_len = gain_row.shape[0]

time: 282 us -> 287 us (1.018)
  matrix products: 49.3 us -> 54.1 us
    dot_general x1 -> x2, matrix products: 24.3 us -> 29.2 us  [shards(): lax.dot_general(tokens_in, piece, (((0,), (0,)), ((), ())), preferred_ele...]
    reduce_scatter x1 -> x2, waiting for transfers between devices: 94.5 us -> 93.8 us  [shards(): lax.psum_scatter(partial_grad, SHARD, scatter_dimension=0, tiled=True)]
  transfers between devices with their start and end apart: 10 -> 11, of which waited for: 10 -> 11; matrix products, arithmetic and copies ran while one was open for 8% -> 14% of each run, Pallas kernels for 0% -> 0%
where the time goes in v2:
time: 287 us; the launch traced here: 286 us
  waiting for transfers between devices  181 us (63%)
  matrix products  54.1 us (19%)
  between operations  17 us (6%)
  other arithmetic  13.7 us (5%)
  starting transfers between devices  12 us (4%)
  local copies, waits for them, and re-layouts  8.22 us (3%)
    reduce_scatter x2, waiting for transfers between devices, shards(): lax.psum_scatter(partial_grad, SHARD, scatter_dimension=0, tiled=True)  93.8 us
    psum x1, waiting for transfers between devices, chip_then_y_sum(): mine = lax.psum(mine, 'chip_y')  44.2 us
    dot_general x2, matrix products, shards(): lax.dot_general(tokens_in, piece, (((0,), (0,)), ((), ())), preferred_ele...  29.2 us
    all_gather x1, waiting for transfers between devices, shards(): refreshed = lax.all_gather(packed_r[:rows_here], SHARD, axis=0, tiled=True)  15.6 us
    ppermute x4, waiting for transfers between devices, butterfly_sum(): x = x + lax.ppermute(x, axis, [(i, i ^ k) for i in range(n)])  14.3 us
    dot_general x5, matrix products, mixer_of(): gram = jnp.dot(current.T, current, precision=ns_mode)  9.45 us
    ppermute x4, starting transfers between devices, butterfly_sum(): x = x + lax.ppermute(x, axis, [(i, i ^ k) for i in range(n)])  8.31 us
    all_gather x1, waiting for transfers between devices, shards(): lax.all_gather(direction, SHARD, axis=0, tiled=True)  7.95 us
  transfers between devices with their start and end apart: 11, of which 11 were waited for; matrix products, arithmetic and copies ran while one was open for 14% of the time, Pallas kernels for 0%

profile of v2, /device:TPU:1, one launch (start us, length us, event | category | flops | bytes accessed | tf_op | source)
XLA Modules:
  0.0 286.3 jit_solution(891678494420767154)
XLA Ops:
  7.2 0.0 reduce-scatter.3.cloned.1.call-start
  7.2 14.6 %fusion.2 = f32[2048,1024]{1,0:T(8,128)} fusion(bf16[1,2048,2048]{2,1,0:T(8,128)(2,1)} %param.12, bf16[2048,2048]{1,0:T(8,128)(2,1)} %bitcast.66), kind=kOutput, calls=%fused_computation.2 | convolution fusion | flops 8589934592 | bytes 20971520 | tf_op jit(solution)/shard_map/dot_general | solution.py:104
  21.9 0.0 reduce-scatter.3.cloned.1.call-update
  21.9 0.0 reduce-scatter.5.cloned.1.call-start
  21.9 14.6 %fusion = f32[2048,1024]{1,0:T(8,128)} fusion(bf16[1,2048,2048]{2,1,0:T(8,128)(2,1)} %param.12, bf16[2048,2048]{1,0:T(8,128)(2,1)} %bitcast.67), kind=kOutput, calls=%fused_computation | convolution fusion | flops 8589934592 | bytes 20971520 | tf_op jit(solution)/shard_map/dot_general | solution.py:104
  36.5 0.0 reduce-scatter.5.cloned.1.call-update
  36.5 0.0 all-reduce.4.cloned.1.call-start
  36.6 40.6 %reduce-scatter.3.cloned.1.call-done = f32[256,1024]{1,0:T(8,128)} async-done(((f32[2048,1024]{1,0:T(8,128)}), f32[256,1024]{1,0:T(8,128)}) %reduce-scatter.3.cloned.1.call-update) | async-done | bytes 1048592 | tf_op jit(solution)/shard_map/reduce_scatter | solution.py:107
  77.2 1.3 constant_dynamic-update-slice_fusion.1
  78.5 53.2 %reduce-scatter.5.cloned.1.call-done = f32[256,1024]{1,0:T(8,128)} async-done(((f32[2048,1024]{1,0:T(8,128)}), f32[256,1024]{1,0:T(8,128)}) %reduce-scatter.5.cloned.1.call-update) | async-done | bytes 1048592 | tf_op jit(solution)/shard_map/reduce_scatter | solution.py:107
  131.7 1.3 constant_dynamic-update-slice_fusion
  133.0 1.1 multiply_reduce_fusion.1
  134.1 2.0 convolution_bitcast_fusion.1
  136.2 0.9 select_maximum_fusion
  137.1 1.4 copy-done.3
  138.5 0.1 constant_dynamic-slice_fusion.1
  138.6 1.3 collective-permute-start
  139.9 2.5 collective-permute-done
  142.4 2.7 dynamic-slice_add_fusion
  145.1 0.2 all-gather.5.cloned.1.call-start
  145.3 44.2 %all-reduce.4.cloned.1.call-done = f32[136,2048]{1,0:T(8,128)} async-done(((f32[136,2048]{1,0:T(8,128)}), f32[136,2048]{1,0:T(8,128)}) %all-reduce.4.cloned.1.call-update) | async-done | bytes 1114128 | tf_op jit(solution)/shard_map/psum | solution.py:76
  189.6 2.1 collective-permute-start.1
  191.6 2.7 collective-permute-done.1
  194.3 1.7 broadcast_select_fusion.1
  196.1 0.6 slice.66
  196.6 1.9 fusion.6
  198.6 0.7 select_maximum_fusion.1
  199.3 1.4 collective-permute-start.2
  200.6 6.4 %collective-permute-done.2 = f32[264,256]{1,0:T(8,128)S(1)} collective-permute-done((f32[264,256]{1,0:T(8,128)S(1)}, f32[264,256]{1,0:T(8,128)S(1)}, u32[]{:S(2)}, u32[]{:S(2)}) %collective-permute-start.2) | collective-permute-done | bytes 270368 | tf_op jit(solution)/shard_map/ppermute | solution.py:64
  207.0 0.7 fusion.28
  207.7 3.0 %collective-permute-start.3 = (f32[264,256]{1,0:T(8,128)S(1)}, f32[264,256]{1,0:T(8,128)S(1)}, u32[]{:S(2)}, u32[]{:S(2)}) collective-permute-start(f32[264,256]{1,0:T(8,128)S(1)} %fusion.28), channel_id=1, source_target_pairs={{0,8},{4,12},{8,0},{12,4},{1,9},{5,13},{9,1},{13,5},{2,10},{6,14},... | collective-permute-start | bytes 811016 | tf_op jit(solution)/shard_map/ppermute | solution.py:64
  210.7 5.4 %collective-permute-done.3 = f32[264,256]{1,0:T(8,128)S(1)} collective-permute-done((f32[264,256]{1,0:T(8,128)S(1)}, f32[264,256]{1,0:T(8,128)S(1)}, u32[]{:S(2)}, u32[]{:S(2)}) %collective-permute-start.3) | collective-permute-done | bytes 270368 | tf_op jit(solution)/shard_map/ppermute | solution.py:64
  216.2 0.7 slice.69
  216.9 0.0 all-gather.3.cloned.1.call-start
  217.0 0.6 fusion.33
  217.6 0.5 slice.67
  219.4 1.3 collective-permute-start.4
  220.7 1.3 collective-permute-done.4
  221.9 2.7 collective-permute-start.5
  224.6 1.2 collective-permute-done.5
  225.9 0.5 slice.62
  227.2 0.8 fusion.20
  227.9 0.9 fusion.19
  228.9 0.6 add_divide_fusion.1
  229.5 15.6 %all-gather.5.cloned.1.call-done = f32[2048,256]{1,0:T(8,128)} async-done(((f32[256,256]{1,0:T(8,128)}), f32[2048,256]{1,0:T(8,128)}) %all-gather.5.cloned.1.call-update) | async-done | bytes 2097168 | tf_op jit(solution)/shard_map/all_gather | solution.py:128
  245.1 2.9 %multiply_reduce_fusion = f32[]{:T(128)} fusion(f32[2048,256]{1,0:T(8,128)} %all-gather.5.cloned.1.call-done), kind=kLoop, calls=%fused_computation.18 | loop fusion | flops 1048575 | bytes 2097156 | tf_op jit(solution)/shard_map/reduce_sum | solution.py:143
  248.7 1.8 fusion.30
  250.5 0.3 fusion.11
  250.8 1.0 fusion.29
  251.8 2.0 fusion.13
  253.8 0.3 fusion.10
  254.1 1.2 convolution_add_fusion.2
  255.3 1.9 fusion.34
  257.2 0.3 fusion.9
  257.5 1.1 convolution_add_fusion.1
  258.6 1.9 fusion.35
  260.7 0.3 fusion.8
  260.9 1.0 convolution_add_fusion
  262.0 1.9 fusion.36
  263.9 0.3 fusion.7
  264.2 0.8 fusion.12
  265.0 8.0 %all-gather.3.cloned.1.call-done = f32[256,2048]{1,0:T(8,128)} async-done(((f32[32,2048]{1,0:T(8,128)}), f32[256,2048]{1,0:T(8,128)}) %all-gather.3.cloned.1.call-update) | async-done | bytes 2097168 | tf_op jit(solution)/shard_map/all_gather | solution.py:140
  273.0 5.0 %convolution_bitcast_fusion = f32[1,256,2048]{1,2,0:T(8,128)S(1)} fusion(f32[256,2048]{1,0:T(8,128)} %all-gather.3.cloned.1.call-done, f32[1,256,256]{2,1,0:T(8,128)S(1)} %copy-done), kind=kOutput, calls=%fused_computation.9 | convolution fusion | flops 1610612736 | bytes 4456448 | tf_op jit(solution)/shard_map/dot_general | solution.py:139
  278.0 1.8 copy.15
  (26 shorter events, 0.1 us)
Async XLA Ops:
  7.2 127.0 %copy-start = (f32[1,256,256]{2,1,0:T(8,128)S(1)}, f32[1,256,256]{2,1,0:T(8,128)}, u32[]{:S(2)}) copy-start(f32[1,256,256]{2,1,0:T(8,128)} %param.14) | copy-start | bytes 786436
  7.2 70.0 %reduce-scatter.3.cloned.1.call-start = ((), (), s32[]{:S(2)}) async-start(), calls=%async_computation.2 | async-start | bytes 9437184 | tf_op jit(solution)/shard_map/reduce_scatter | solution.py:107
  21.9 109.8 %reduce-scatter.5.cloned.1.call-start = ((), (), s32[]{:S(2)}) async-start(), calls=%async_computation.3 | async-start | bytes 9437184 | tf_op jit(solution)/shard_map/reduce_scatter | solution.py:107
  36.5 153.0 %all-reduce.4.cloned.1.call-start = ((), (), s32[]{:S(2)}) async-start(), calls=%async_computation.4 | async-start | bytes 2228224 | tf_op jit(solution)/shard_map/psum | solution.py:76
  134.1 2.1 copy-start.7
  137.1 1.4 copy-start.3
  138.6 3.8 %collective-permute-start = (f32[136,2048]{1,0:T(8,128)S(1)}, f32[136,2048]{1,0:T(8,128)}, u32[]{:S(2)}, u32[]{:S(2)}) collective-permute-start(f32[136,2048]{1,0:T(8,128)S(1)} %constant_dynamic-slice_fusion.1), channel_id=1, source_target_pairs={{0,16},{16,0},{1,17},{17,1},{2,18},{18,2},{3,19},{19,3},{4,20},{20... | collective-permute-start | bytes 3342344 | tf_op jit(solution)/shard_map/ppermute | solution.py:75
  145.1 100.0 %all-gather.5.cloned.1.call-start = ((), (), s32[]{:S(2)}) async-start(), calls=%async_computation.6 | async-start | bytes 2359296 | tf_op jit(solution)/shard_map/all_gather | solution.py:128
  189.6 4.8 %collective-permute-start.1 = (f32[136,2048]{1,0:T(8,128)}, f32[136,2048]{1,0:T(8,128)}, u32[]{:S(2)}, u32[]{:S(2)}) collective-permute-start(f32[136,2048]{1,0:T(8,128)} %all-reduce.4.cloned.1.call-done), channel_id=1, source_target_pairs={{0,16},{16,0},{1,17},{17,1},{2,18},{18,2},{3,19},{19,3},{4,20},{20... | collective-permute-start | bytes 3342344 | tf_op jit(solution)/shard_map/ppermute | solution.py:77
  196.1 2.5 copy-start.1
  198.5 28.6 %copy-start.5 = (f32[1,32,2048]{2,1,0:T(8,128)S(1)}, f32[1,32,2048]{2,1,0:T(8,128)}, u32[]{:S(2)}) copy-start(f32[1,32,2048]{2,1,0:T(8,128)} %param.16) | copy-start | bytes 786436
  199.3 27.8 %copy-start.2 = (f32[136,2048]{1,0:T(8,128)S(1)}, f32[136,2048]{1,0:T(8,128)}, u32[]{:S(2)}) copy-start(f32[136,2048]{1,0:T(8,128)} %copy-done.1) | copy-start | bytes 3342340
  199.3 7.7 %collective-permute-start.2 = (f32[264,256]{1,0:T(8,128)S(1)}, f32[264,256]{1,0:T(8,128)S(1)}, u32[]{:S(2)}, u32[]{:S(2)}) collective-permute-start(f32[264,256]{1,0:T(8,128)S(1)} %select_maximum_fusion.1), channel_id=1, source_target_pairs={{0,4},{4,0},{8,12},{12,8},{1,5},{5,1},{9,13},{13,9},{2,6},{6,2},{1... | collective-permute-start | bytes 811016 | tf_op jit(solution)/shard_map/ppermute | solution.py:64
  207.7 8.4 %collective-permute-start.3 = (f32[264,256]{1,0:T(8,128)S(1)}, f32[264,256]{1,0:T(8,128)S(1)}, u32[]{:S(2)}, u32[]{:S(2)}) collective-permute-start(f32[264,256]{1,0:T(8,128)S(1)} %fusion.28), channel_id=1, source_target_pairs={{0,8},{4,12},{8,0},{12,4},{1,9},{5,13},{9,1},{13,5},{2,10},{6,14},... | collective-permute-start | bytes 811016 | tf_op jit(solution)/shard_map/ppermute | solution.py:64
  216.1 11.8 %copy-start.6 = (f32[1,32,2048]{2,1,0:T(8,128)S(1)}, f32[1,32,2048]{2,1,0:T(8,128)}, u32[]{:S(2)}) copy-start(f32[1,32,2048]{2,1,0:T(8,128)} %param.15) | copy-start | bytes 786436
  216.9 56.0 %all-gather.3.cloned.1.call-start = ((), (), s32[]{:S(2)}) async-start(), calls=%async_computation.5 | async-start | bytes 2359296 | tf_op jit(solution)/shard_map/all_gather | solution.py:140
  219.4 2.5 collective-permute-start.4
  221.9 4.0 %collective-permute-start.5 = (f32[8,128]{1,0:T(8,128)S(1)}, f32[8,128]{1,0:T(8,128)S(1)}, u32[]{:S(2)}, u32[]{:S(2)}) collective-permute-start(f32[8,128]{1,0:T(8,128)S(1)} %broadcast_add_fusion), channel_id=1, source_target_pairs={{0,2},{1,3},{2,0},{3,1},{4,6},{5,7},{6,4},{7,5},{8,10},{9,11},{10,... | collective-permute-start | bytes 12296 | tf_op jit(solution)/shard_map/ppermute | solution.py:64
  227.1 1.8 copy-start.8
  227.1 1.8 copy-start.9
  245.1 3.6 %copy-start.4 = (f32[2048,256]{1,0:T(8,128)S(1)}, f32[2048,256]{1,0:T(8,128)}, u32[]{:S(2)}) copy-start(f32[2048,256]{1,0:T(8,128)} %all-gather.5.cloned.1.call-done) | copy-start | bytes 6291460
Sparse Core Ops, SparseCore 0:
  22.0 55.1 reduce-scatter.2
  79.6 52.0 reduce-scatter.4
  145.2 44.2 all-reduce.3
  217.0 28.0 all-gather.4
  247.2 25.6 all-gather.2

commit v3 on v0

--- a/solution.py
+++ b/solution.py
@@ -121,7 +121,11 @@
     extra_r = jnp.zeros((PAD, rank), jnp.float32).at[0, 0].set(square_shard)
     packed_r = butterfly_sum(jnp.concatenate([refresh_part, extra_r], axis=0), "tensor")
     square_st = packed_r[rows_here, 0]
-    refreshed = lax.all_gather(packed_r[:rows_here], SHARD, axis=0, tiled=True)
+    refresh_rows = packed_r[:rows_here]
+    frob_row = jnp.zeros((PAD, rank), jnp.float32).at[0, 0].set(jnp.sum(refresh_rows * refresh_rows))
+    gathered = lax.all_gather(jnp.concatenate([refresh_rows, frob_row], 0), SHARD, axis=0, tiled=False)
+    refreshed = gathered[:, :rows_here].reshape(shard_count * rows_here, rank)
+    frob = jnp.sum(gathered[:, rows_here, 0])
 
     gain_own = lax.dynamic_slice_in_dim(gain_total, shard_pos * rows_here, rows_here, 0)
     square_local = square_st + jnp.sum(gain_total * gain_total)
@@ -133,10 +137,10 @@
         clip * proj_rows, first_moment[layer_index], second_moment[layer_index]
     )
     update_here = jnp.dot(
-        basis_here, lax.all_gather(direction, SHARD, axis=0, tiled=True), precision=exact_mode
-    )
-
-    current = refreshed / jnp.sqrt(jnp.sum(refreshed * refreshed) + ns_eps)
+        basis_here, lax.all_gather(direction, SHARD, axis=0, tiled=True), precision=ns_mode
+    )
+
+    current = refreshed / jnp.sqrt(frob + ns_eps)
     for step_index in range(NS_STEPS - 1):
         current = coef_first * current + jnp.dot(current, mixer_of(current), precision=ns_mode)
     row_start = shard_pos * rows_here + tensor_pos * out_rows

time: 282 us -> 307 us (1.089)
  waiting for transfers between devices: 182 us -> 208 us
    all_gather x1, waiting for transfers between devices: 7.96 us -> 27.7 us  [shards(): lax.all_gather(direction, SHARD, axis=0, tiled=True)]
    all_gather x1, waiting for transfers between devices: 15.6 us -> 22.1 us  [shards(): lax.all_gather(jnp.concatenate([refresh_rows, frob_row], 0), SHARD, axis=...]
  transfers between devices with their start and end apart: 10 -> 10, of which waited for: 10 -> 10; matrix products, arithmetic and copies ran while one was open for 8% -> 3% of each run, Pallas kernels for 0% -> 0%
where the time goes in v3:
time: 307 us
  waiting for transfers between devices  208 us (68%)
  matrix products  47.7 us (16%)
  other arithmetic  17.8 us (6%)
  between operations  16.8 us (5%)
  starting transfers between devices  11.8 us (4%)
  local copies, waits for them, and re-layouts  4.91 us (2%)
    reduce_scatter x1, waiting for transfers between devices, shards(): lax.psum_scatter(partial_grad, SHARD, scatter_dimension=0, tiled=True)  94.5 us
    psum x1, waiting for transfers between devices, chip_then_y_sum(): mine = lax.psum(mine, 'chip_y')  44.4 us
    all_gather x1, waiting for transfers between devices, shards(): lax.all_gather(direction, SHARD, axis=0, tiled=True)  27.7 us
    dot_general x1, matrix products, shards(): lax.dot_general(tokens_in, grads_out, (((0,), (0,)), ((), ())), preferred...  24.4 us
    all_gather x1, waiting for transfers between devices, shards(): lax.all_gather(jnp.concatenate([refresh_rows, frob_row], 0), SHARD, axis=...  22.1 us
    ppermute x4, waiting for transfers between devices, butterfly_sum(): x = x + lax.ppermute(x, axis, [(i, i ^ k) for i in range(n)])  13.7 us
    dot_general x5, matrix products, mixer_of(): gram = jnp.dot(current.T, current, precision=ns_mode)  9.37 us
    ppermute x4, starting transfers between devices, butterfly_sum(): x = x + lax.ppermute(x, axis, [(i, i ^ k) for i in range(n)])  8.29 us
  transfers between devices with their start and end apart: 10, of which 10 were waited for; matrix products, arithmetic and copies ran while one was open for 3% of the time, Pallas kernels for 0%

profile of v3, /device:TPU:1, one launch (start us, length us, event | category | flops | bytes accessed | tf_op | source)
XLA Modules:
  0.0 306.8 jit_solution(4854795875515189235)
XLA Ops:
  7.2 0.0 copy-start
  7.2 0.0 reduce-scatter.2.cloned.1.call-start
  7.2 24.4 %fusion = f32[2048,2048]{1,0:T(8,128)} fusion(bf16[1,2048,2048]{2,1,0:T(8,128)(2,1)} %param.15, bf16[1,2048,2048]{2,1,0:T(8,128)(2,1)} %param.14), kind=kOutput, calls=%fused_computation | convolution fusion | flops 17179869184 | bytes 33554432 | tf_op jit(solution)/shard_map/dot_general | solution.py:101
  31.6 0.0 reduce-scatter.2.cloned.1.call-update
  31.7 0.0 all-reduce.5.cloned.1.call-start
  31.7 94.5 %reduce-scatter.2.cloned.1.call-done = f32[256,2048]{1,0:T(8,128)} async-done(((f32[2048,2048]{1,0:T(8,128)}), f32[256,2048]{1,0:T(8,128)}) %reduce-scatter.2.cloned.1.call-update) | async-done | bytes 2097168 | tf_op jit(solution)/shard_map/reduce_scatter | solution.py:104
  126.3 2.9 multiply_reduce_fusion
  129.1 2.0 convolution_bitcast_fusion.1
  131.2 0.9 select_maximum_fusion
  132.1 1.4 copy-done.4
  133.5 0.1 constant_dynamic-slice_fusion.1
  133.6 1.3 collective-permute-start
  134.9 2.5 collective-permute-done
  137.4 2.7 dynamic-slice_add_fusion
  140.1 0.0 all-reduce.5.cloned.1.call-update
  140.1 0.0 all-gather.4.cloned.1.call-start
  140.2 44.4 %all-reduce.5.cloned.1.call-done = f32[136,2048]{1,0:T(8,128)} async-done(((f32[136,2048]{1,0:T(8,128)}), f32[136,2048]{1,0:T(8,128)}) %all-reduce.5.cloned.1.call-update) | async-done | bytes 1114128 | tf_op jit(solution)/shard_map/psum | solution.py:76
  184.6 2.1 collective-permute-start.1
  186.6 2.7 collective-permute-done.1
  189.4 1.7 broadcast_select_fusion.1
  191.1 0.5 slice.80
  191.7 1.9 fusion.3
  193.6 0.7 select_maximum_fusion.2
  194.3 1.4 collective-permute-start.2
  195.7 6.4 %collective-permute-done.2 = f32[264,256]{1,0:T(8,128)S(1)} collective-permute-done((f32[264,256]{1,0:T(8,128)S(1)}, f32[264,256]{1,0:T(8,128)S(1)}, u32[]{:S(2)}, u32[]{:S(2)}) %collective-permute-start.2) | collective-permute-done | bytes 270368 | tf_op jit(solution)/shard_map/ppermute | solution.py:64
  202.0 0.7 fusion.22
  202.7 3.0 collective-permute-start.3
  205.7 0.6 fusion.25
  206.3 4.8 %collective-permute-done.3 = f32[264,256]{1,0:T(8,128)S(1)} collective-permute-done((f32[264,256]{1,0:T(8,128)S(1)}, f32[264,256]{1,0:T(8,128)S(1)}, u32[]{:S(2)}, u32[]{:S(2)}) %collective-permute-start.3) | collective-permute-done | bytes 270368 | tf_op jit(solution)/shard_map/ppermute | solution.py:64
  211.2 0.5 slice.81
  213.0 1.3 collective-permute-start.4
  214.3 1.3 collective-permute-done.4
  215.5 2.7 collective-permute-start.5
  218.2 1.3 collective-permute-done.5
  219.5 0.5 slice.76
  220.7 0.8 fusion.16
  221.5 0.9 fusion.15
  222.5 0.0 all-gather.4.cloned.1.call-update
  222.5 0.0 all-gather.6.cloned.1.call-start
  222.5 0.7 fusion.26
  223.2 1.4 select_maximum_fusion.1
  224.6 0.0 all-gather.6.cloned.1.call-update
  224.7 0.6 add_divide_fusion.1
  225.3 27.7 %all-gather.4.cloned.1.call-done = f32[256,2048]{1,0:T(8,128)} async-done(((f32[32,2048]{1,0:T(8,128)}), f32[256,2048]{1,0:T(8,128)}) %all-gather.4.cloned.1.call-update) | async-done | bytes 2097168 | tf_op jit(solution)/shard_map/all_gather | solution.py:140
  253.0 3.4 %convolution_bitcast_fusion = f32[1,256,2048]{1,2,0:T(8,128)S(1)} fusion(f32[256,2048]{1,0:T(8,128)} %all-gather.4.cloned.1.call-done, f32[1,256,256]{2,1,0:T(8,128)S(1)} %copy-done), kind=kOutput, calls=%fused_computation.7 | convolution fusion | flops 805306368 | bytes 4456448 | tf_op jit(solution)/shard_map/dot_general | solution.py:139
  256.4 1.8 copy.16
  258.2 22.1 %all-gather.6.cloned.1.call-done = f32[2112,256]{1,0:T(8,128)} async-done(((f32[264,256]{1,0:T(8,128)}), f32[2112,256]{1,0:T(8,128)}) %all-gather.6.cloned.1.call-update) | async-done | bytes 2162704 | tf_op jit(solution)/shard_map/all_gather | solution.py:126
  280.3 1.4 slice_reduce_fusion
  282.4 1.8 slice_divide_fusion
  284.2 1.9 convolution_bitcast_fusion.2
  286.1 0.3 fusion.8
  286.3 1.0 convolution_add_fusion.3
  287.4 1.9 fusion.27
  289.3 0.3 fusion.7
  289.6 1.0 convolution_add_fusion.2
  290.6 1.9 fusion.28
  292.5 0.3 fusion.6
  292.8 1.0 convolution_add_fusion.1
  293.8 1.9 fusion.29
  295.7 0.3 fusion.5
  296.0 1.3 convolution_add_fusion
  297.2 1.9 fusion.30
  299.1 0.3 fusion.4
  299.4 0.8 fusion.9
  (22 shorter events, 0.1 us)
Async XLA Ops:
  7.2 122.0 %copy-start = (f32[1,256,256]{2,1,0:T(8,128)S(1)}, f32[1,256,256]{2,1,0:T(8,128)}, u32[]{:S(2)}) copy-start(f32[1,256,256]{2,1,0:T(8,128)} %param.16) | copy-start | bytes 786436
  7.2 119.1 %reduce-scatter.2.cloned.1.call-start = ((), (), s32[]{:S(2)}) async-start(), calls=%async_computation.1 | async-start | bytes 18874368 | tf_op jit(solution)/shard_map/reduce_scatter | solution.py:104
  31.7 152.9 %all-reduce.5.cloned.1.call-start = ((), (), s32[]{:S(2)}) async-start(), calls=%async_computation.2 | async-start | bytes 2228224 | tf_op jit(solution)/shard_map/psum | solution.py:76
  126.3 2.9 copy-start.1
  129.1 2.0 copy-start.7
  132.1 1.4 copy-start.4
  133.6 3.8 %collective-permute-start = (f32[136,2048]{1,0:T(8,128)S(1)}, f32[136,2048]{1,0:T(8,128)}, u32[]{:S(2)}, u32[]{:S(2)}) collective-permute-start(f32[136,2048]{1,0:T(8,128)S(1)} %constant_dynamic-slice_fusion.1), channel_id=1, source_target_pairs={{0,16},{16,0},{1,17},{17,1},{2,18},{18,2},{3,19},{19,3},{4,20},{20... | collective-permute-start | bytes 3342344 | tf_op jit(solution)/shard_map/ppermute | solution.py:75
  140.1 112.9 %all-gather.4.cloned.1.call-start = ((), (), s32[]{:S(2)}) async-start(), calls=%async_computation.3 | async-start | bytes 2359296 | tf_op jit(solution)/shard_map/all_gather | solution.py:140
  184.6 4.8 %collective-permute-start.1 = (f32[136,2048]{1,0:T(8,128)}, f32[136,2048]{1,0:T(8,128)}, u32[]{:S(2)}, u32[]{:S(2)}) collective-permute-start(f32[136,2048]{1,0:T(8,128)} %all-reduce.5.cloned.1.call-done), channel_id=1, source_target_pairs={{0,16},{16,0},{1,17},{17,1},{2,18},{18,2},{3,19},{19,3},{4,20},{20... | collective-permute-start | bytes 3342344 | tf_op jit(solution)/shard_map/ppermute | solution.py:77
  191.1 2.4 copy-start.2
  193.6 27.2 %copy-start.5 = (f32[1,32,2048]{2,1,0:T(8,128)S(1)}, f32[1,32,2048]{2,1,0:T(8,128)}, u32[]{:S(2)}) copy-start(f32[1,32,2048]{2,1,0:T(8,128)} %param.18) | copy-start | bytes 786436
  194.3 26.4 %copy-start.3 = (f32[136,2048]{1,0:T(8,128)S(1)}, f32[136,2048]{1,0:T(8,128)}, u32[]{:S(2)}) copy-start(f32[136,2048]{1,0:T(8,128)} %copy-done.2) | copy-start | bytes 3342340
  194.3 7.7 %collective-permute-start.2 = (f32[264,256]{1,0:T(8,128)S(1)}, f32[264,256]{1,0:T(8,128)S(1)}, u32[]{:S(2)}, u32[]{:S(2)}) collective-permute-start(f32[264,256]{1,0:T(8,128)S(1)} %select_maximum_fusion.2), channel_id=1, source_target_pairs={{0,4},{4,0},{8,12},{12,8},{1,5},{5,1},{9,13},{13,9},{2,6},{6,2},{1... | collective-permute-start | bytes 811016 | tf_op jit(solution)/shard_map/ppermute | solution.py:64
  202.7 18.8 %copy-start.6 = (f32[1,32,2048]{2,1,0:T(8,128)S(1)}, f32[1,32,2048]{2,1,0:T(8,128)}, u32[]{:S(2)}) copy-start(f32[1,32,2048]{2,1,0:T(8,128)} %param.17) | copy-start | bytes 786436
  202.7 8.4 %collective-permute-start.3 = (f32[264,256]{1,0:T(8,128)S(1)}, f32[264,256]{1,0:T(8,128)S(1)}, u32[]{:S(2)}, u32[]{:S(2)}) collective-permute-start(f32[264,256]{1,0:T(8,128)S(1)} %fusion.22), channel_id=1, source_target_pairs={{0,8},{4,12},{8,0},{12,4},{1,9},{5,13},{9,1},{13,5},{2,10},{6,14},... | collective-permute-start | bytes 811016 | tf_op jit(solution)/shard_map/ppermute | solution.py:64
  213.0 2.5 collective-permute-start.4
  215.5 4.0 %collective-permute-start.5 = (f32[8,128]{1,0:T(8,128)S(1)}, f32[8,128]{1,0:T(8,128)S(1)}, u32[]{:S(2)}, u32[]{:S(2)}) collective-permute-start(f32[8,128]{1,0:T(8,128)S(1)} %broadcast_add_fusion), channel_id=1, source_target_pairs={{0,2},{1,3},{2,0},{3,1},{4,6},{5,7},{6,4},{7,5},{8,10},{9,11},{10,... | collective-permute-start | bytes 12296 | tf_op jit(solution)/shard_map/ppermute | solution.py:64
  221.5 3.1 %copy-start.8 = (f32[1,256]{1,0:T(1,128)S(1)}, f32[1,256]{1,0:T(1,128)}, u32[]{:S(2)}) copy-start(f32[1,256]{1,0:T(1,128)} %param.20) | copy-start | bytes 3076
  221.5 3.1 %copy-start.9 = (f32[1,256]{1,0:T(1,128)S(1)}, f32[1,256]{1,0:T(1,128)}, u32[]{:S(2)}) copy-start(f32[1,256]{1,0:T(1,128)} %param.21) | copy-start | bytes 3076
  222.5 57.8 %all-gather.6.cloned.1.call-start = ((), (), s32[]{:S(2)}) async-start(), calls=%async_computation.4 | async-start | bytes 2433024 | tf_op jit(solution)/shard_map/all_gather | solution.py:126
Sparse Core Ops, SparseCore 0:
  31.8 94.4 reduce-scatter.1
  140.3 44.2 all-reduce.4
  222.6 30.3 all-gather.3
  254.5 25.7 all-gather.5

commit v4 on v3

--- a/solution.py
+++ b/solution.py
@@ -136,8 +136,9 @@
     first_new, second_new, direction = adam_direction(
         clip * proj_rows, first_moment[layer_index], second_moment[layer_index]
     )
+    direction_sent = direction + 0.0 * frob
     update_here = jnp.dot(
-        basis_here, lax.all_gather(direction, SHARD, axis=0, tiled=True), precision=ns_mode
+        basis_here, lax.all_gather(direction_sent, SHARD, axis=0, tiled=True), precision=ns_mode
     )
 
     current = refreshed / jnp.sqrt(frob + ns_eps)

time: 307 us -> 287 us (0.935)
  waiting for transfers between devices: 208 us -> 187 us
    all_gather x1, waiting for transfers between devices: 27.7 us -> 11.9 us  [shards(): lax.all_gather(direction_sent, SHARD, axis=0, tiled=True)]
    all_gather x1, waiting for transfers between devices: 22.1 us -> 16.7 us  [shards(): lax.all_gather(jnp.concatenate([refresh_rows, frob_row], 0), SHARD, axis=...]
  transfers between devices with their start and end apart: 10 -> 10, of which waited for: 10 -> 10; matrix products, arithmetic and copies ran while one was open for 3% -> 6% of each run, Pallas kernels for 0% -> 0%
where the time goes in v4:
time: 287 us
  waiting for transfers between devices  187 us (65%)
  matrix products  47.6 us (17%)
  other arithmetic  17.8 us (6%)
  between operations  17.4 us (6%)
  starting transfers between devices  11.8 us (4%)
  local copies, waits for them, and re-layouts  4.91 us (2%)
    reduce_scatter x1, waiting for transfers between devices, shards(): lax.psum_scatter(partial_grad, SHARD, scatter_dimension=0, tiled=True)  94.5 us
    psum x1, waiting for transfers between devices, chip_then_y_sum(): mine = lax.psum(mine, 'chip_y')  44.4 us
    dot_general x1, matrix products, shards(): lax.dot_general(tokens_in, grads_out, (((0,), (0,)), ((), ())), preferred...  24.4 us
    all_gather x1, waiting for transfers between devices, shards(): lax.all_gather(jnp.concatenate([refresh_rows, frob_row], 0), SHARD, axis=...  16.7 us
    ppermute x4, waiting for transfers between devices, butterfly_sum(): x = x + lax.ppermute(x, axis, [(i, i ^ k) for i in range(n)])  14.3 us
    all_gather x1, waiting for transfers between devices, shards(): lax.all_gather(direction_sent, SHARD, axis=0, tiled=True)  11.9 us
    dot_general x5, matrix products, mixer_of(): gram = jnp.dot(current.T, current, precision=ns_mode)  9.3 us
    ppermute x4, starting transfers between devices, butterfly_sum(): x = x + lax.ppermute(x, axis, [(i, i ^ k) for i in range(n)])  8.3 us
  transfers between devices with their start and end apart: 10, of which 10 were waited for; matrix products, arithmetic and copies ran while one was open for 6% of the time, Pallas kernels for 0%

profile of v4, /device:TPU:1, one launch (start us, length us, event | category | flops | bytes accessed | tf_op | source)
XLA Modules:
  0.0 286.8 jit_solution(8171240495104158617)
XLA Ops:
  7.2 0.0 copy-start
  7.2 0.0 reduce-scatter.2.cloned.1.call-start
  7.2 24.4 %fusion = f32[2048,2048]{1,0:T(8,128)} fusion(bf16[1,2048,2048]{2,1,0:T(8,128)(2,1)} %param.15, bf16[1,2048,2048]{2,1,0:T(8,128)(2,1)} %param.14), kind=kOutput, calls=%fused_computation | convolution fusion | flops 17179869184 | bytes 33554432 | tf_op jit(solution)/shard_map/dot_general | solution.py:101
  31.6 0.0 reduce-scatter.2.cloned.1.call-update
  31.7 0.0 all-reduce.5.cloned.1.call-start
  31.7 94.5 %reduce-scatter.2.cloned.1.call-done = f32[256,2048]{1,0:T(8,128)} async-done(((f32[2048,2048]{1,0:T(8,128)}), f32[256,2048]{1,0:T(8,128)}) %reduce-scatter.2.cloned.1.call-update) | async-done | bytes 2097168 | tf_op jit(solution)/shard_map/reduce_scatter | solution.py:104
  126.3 2.9 %multiply_reduce_fusion = f32[]{:T(128)} fusion(f32[256,2048]{1,0:T(8,128)} %reduce-scatter.2.cloned.1.call-done), kind=kLoop, calls=%fused_computation.16 | loop fusion | flops 1048575 | bytes 2097156 | tf_op jit(solution)/shard_map/reduce_sum | solution.py:110
  129.1 2.0 convolution_bitcast_fusion.1
  131.2 0.9 select_maximum_fusion
  132.1 1.4 copy-done.4
  133.5 0.1 constant_dynamic-slice_fusion.1
  133.6 1.3 collective-permute-start
  134.9 2.5 collective-permute-done
  137.4 2.7 dynamic-slice_add_fusion
  140.1 0.0 all-reduce.5.cloned.1.call-update
  140.1 0.0 all-gather.6.cloned.1.call-start
  140.2 44.4 %all-reduce.5.cloned.1.call-done = f32[136,2048]{1,0:T(8,128)} async-done(((f32[136,2048]{1,0:T(8,128)}), f32[136,2048]{1,0:T(8,128)}) %all-reduce.5.cloned.1.call-update) | async-done | bytes 1114128 | tf_op jit(solution)/shard_map/psum | solution.py:76
  184.6 2.1 collective-permute-start.1
  186.7 2.7 collective-permute-done.1
  189.4 1.7 broadcast_select_fusion.1
  191.1 0.5 slice.80
  191.7 1.9 fusion.3
  193.6 0.7 select_maximum_fusion.2
  194.3 1.4 collective-permute-start.2
  195.7 6.4 %collective-permute-done.2 = f32[264,256]{1,0:T(8,128)S(1)} collective-permute-done((f32[264,256]{1,0:T(8,128)S(1)}, f32[264,256]{1,0:T(8,128)S(1)}, u32[]{:S(2)}, u32[]{:S(2)}) %collective-permute-start.2) | collective-permute-done | bytes 270368 | tf_op jit(solution)/shard_map/ppermute | solution.py:64
  202.1 0.7 fusion.22
  202.8 3.0 %collective-permute-start.3 = (f32[264,256]{1,0:T(8,128)S(1)}, f32[264,256]{1,0:T(8,128)S(1)}, u32[]{:S(2)}, u32[]{:S(2)}) collective-permute-start(f32[264,256]{1,0:T(8,128)S(1)} %fusion.22), channel_id=1, source_target_pairs={{0,8},{4,12},{8,0},{12,4},{1,9},{5,13},{9,1},{13,5},{2,10},{6,14},... | collective-permute-start | bytes 811016 | tf_op jit(solution)/shard_map/ppermute | solution.py:64
  205.7 5.4 %collective-permute-done.3 = f32[264,256]{1,0:T(8,128)S(1)} collective-permute-done((f32[264,256]{1,0:T(8,128)S(1)}, f32[264,256]{1,0:T(8,128)S(1)}, u32[]{:S(2)}, u32[]{:S(2)}) %collective-permute-start.3) | collective-permute-done | bytes 270368 | tf_op jit(solution)/shard_map/ppermute | solution.py:64
  211.2 0.7 fusion.26
  211.9 1.4 select_maximum_fusion.1
  213.2 0.0 all-gather.6.cloned.1.call-update
  213.2 0.0 all-gather.4.cloned.1.call-start
  213.3 0.6 fusion.25
  213.9 0.5 slice.81
  215.7 1.3 collective-permute-start.4
  217.0 1.3 collective-permute-done.4
  218.3 2.7 collective-permute-start.5
  221.0 1.3 collective-permute-done.5
  222.2 0.5 slice.76
  223.5 0.6 add_divide_fusion
  224.1 0.8 fusion.16
  224.9 16.7 %all-gather.6.cloned.1.call-done = f32[2112,256]{1,0:T(8,128)} async-done(((f32[264,256]{1,0:T(8,128)}), f32[2112,256]{1,0:T(8,128)}) %all-gather.6.cloned.1.call-update) | async-done | bytes 2162704 | tf_op jit(solution)/shard_map/all_gather | solution.py:126
  241.5 1.4 slice_reduce_fusion
  243.6 1.8 slice_divide_fusion
  245.4 1.8 convolution_bitcast_fusion.2
  247.2 0.3 fusion.8
  248.2 1.0 fusion.15
  249.1 0.0 all-gather.4.cloned.1.call-update
  249.2 1.0 convolution_add_fusion.3
  250.2 1.9 fusion.27
  252.1 0.3 fusion.7
  252.4 1.0 convolution_add_fusion.2
  253.4 1.9 fusion.28
  255.3 0.3 fusion.6
  255.6 1.0 convolution_add_fusion.1
  256.6 1.9 fusion.29
  258.5 0.3 fusion.5
  258.8 1.3 convolution_add_fusion
  260.1 1.9 fusion.30
  261.9 0.3 fusion.4
  262.2 0.8 fusion.9
  263.1 11.9 %all-gather.4.cloned.1.call-done = f32[256,2048]{1,0:T(8,128)} async-done(((f32[32,2048]{1,0:T(8,128)}), f32[256,2048]{1,0:T(8,128)}) %all-gather.4.cloned.1.call-update) | async-done | bytes 2097168 | tf_op jit(solution)/shard_map/all_gather | solution.py:141
  275.0 3.4 %convolution_bitcast_fusion = f32[1,256,2048]{1,2,0:T(8,128)S(1)} fusion(f32[256,2048]{1,0:T(8,128)} %all-gather.4.cloned.1.call-done, f32[1,256,256]{2,1,0:T(8,128)S(1)} %copy-done), kind=kOutput, calls=%fused_computation.7 | convolution fusion | flops 805306368 | bytes 4456448 | tf_op jit(solution)/shard_map/dot_general | solution.py:140
  278.4 1.8 copy.16
  (22 shorter events, 0.1 us)
Async XLA Ops:
  7.2 122.0 %copy-start = (f32[1,256,256]{2,1,0:T(8,128)S(1)}, f32[1,256,256]{2,1,0:T(8,128)}, u32[]{:S(2)}) copy-start(f32[1,256,256]{2,1,0:T(8,128)} %param.16) | copy-start | bytes 786436
  7.2 119.1 %reduce-scatter.2.cloned.1.call-start = ((), (), s32[]{:S(2)}) async-start(), calls=%async_computation.1 | async-start | bytes 18874368 | tf_op jit(solution)/shard_map/reduce_scatter | solution.py:104
  31.7 152.9 %all-reduce.5.cloned.1.call-start = ((), (), s32[]{:S(2)}) async-start(), calls=%async_computation.2 | async-start | bytes 2228224 | tf_op jit(solution)/shard_map/psum | solution.py:76
  126.3 2.9 %copy-start.1 = (f32[256,2048]{1,0:T(8,128)S(1)}, f32[256,2048]{1,0:T(8,128)}, u32[]{:S(2)}) copy-start(f32[256,2048]{1,0:T(8,128)} %reduce-scatter.2.cloned.1.call-done) | copy-start | bytes 6291460
  129.1 2.0 copy-start.7
  132.1 1.4 copy-start.4
  133.6 3.8 %collective-permute-start = (f32[136,2048]{1,0:T(8,128)S(1)}, f32[136,2048]{1,0:T(8,128)}, u32[]{:S(2)}, u32[]{:S(2)}) collective-permute-start(f32[136,2048]{1,0:T(8,128)S(1)} %constant_dynamic-slice_fusion.1), channel_id=1, source_target_pairs={{0,16},{16,0},{1,17},{17,1},{2,18},{18,2},{3,19},{19,3},{4,20},{20... | collective-permute-start | bytes 3342344 | tf_op jit(solution)/shard_map/ppermute | solution.py:75
  140.1 101.4 %all-gather.6.cloned.1.call-start = ((), (), s32[]{:S(2)}) async-start(), calls=%async_computation.4 | async-start | bytes 2433024 | tf_op jit(solution)/shard_map/all_gather | solution.py:126
  184.6 4.8 %collective-permute-start.1 = (f32[136,2048]{1,0:T(8,128)}, f32[136,2048]{1,0:T(8,128)}, u32[]{:S(2)}, u32[]{:S(2)}) collective-permute-start(f32[136,2048]{1,0:T(8,128)} %all-reduce.5.cloned.1.call-done), channel_id=1, source_target_pairs={{0,16},{16,0},{1,17},{17,1},{2,18},{18,2},{3,19},{19,3},{4,20},{20... | collective-permute-start | bytes 3342344 | tf_op jit(solution)/shard_map/ppermute | solution.py:77
  191.1 2.4 copy-start.2
  193.6 29.9 %copy-start.8 = (f32[1,256]{1,0:T(1,128)S(1)}, f32[1,256]{1,0:T(1,128)}, u32[]{:S(2)}) copy-start(f32[1,256]{1,0:T(1,128)} %param.20) | copy-start | bytes 3076
  193.6 29.9 %copy-start.9 = (f32[1,256]{1,0:T(1,128)S(1)}, f32[1,256]{1,0:T(1,128)}, u32[]{:S(2)}) copy-start(f32[1,256]{1,0:T(1,128)} %param.21) | copy-start | bytes 3076
  193.6 30.5 %copy-start.5 = (f32[1,32,2048]{2,1,0:T(8,128)S(1)}, f32[1,32,2048]{2,1,0:T(8,128)}, u32[]{:S(2)}) copy-start(f32[1,32,2048]{2,1,0:T(8,128)} %param.18) | copy-start | bytes 786436
  194.3 29.8 %copy-start.3 = (f32[136,2048]{1,0:T(8,128)S(1)}, f32[136,2048]{1,0:T(8,128)}, u32[]{:S(2)}) copy-start(f32[136,2048]{1,0:T(8,128)} %copy-done.2) | copy-start | bytes 3342340
  194.3 7.7 %collective-permute-start.2 = (f32[264,256]{1,0:T(8,128)S(1)}, f32[264,256]{1,0:T(8,128)S(1)}, u32[]{:S(2)}, u32[]{:S(2)}) collective-permute-start(f32[264,256]{1,0:T(8,128)S(1)} %select_maximum_fusion.2), channel_id=1, source_target_pairs={{0,4},{4,0},{8,12},{12,8},{1,5},{5,1},{9,13},{13,9},{2,6},{6,2},{1... | collective-permute-start | bytes 811016 | tf_op jit(solution)/shard_map/ppermute | solution.py:64
  202.8 8.4 %collective-permute-start.3 = (f32[264,256]{1,0:T(8,128)S(1)}, f32[264,256]{1,0:T(8,128)S(1)}, u32[]{:S(2)}, u32[]{:S(2)}) collective-permute-start(f32[264,256]{1,0:T(8,128)S(1)} %fusion.22), channel_id=1, source_target_pairs={{0,8},{4,12},{8,0},{12,4},{1,9},{5,13},{9,1},{13,5},{2,10},{6,14},... | collective-permute-start | bytes 811016 | tf_op jit(solution)/shard_map/ppermute | solution.py:64
  213.2 61.8 %all-gather.4.cloned.1.call-start = ((), (), s32[]{:S(2)}) async-start(), calls=%async_computation.3 | async-start | bytes 2359296 | tf_op jit(solution)/shard_map/all_gather | solution.py:141
  215.7 2.5 collective-permute-start.4
  218.3 4.0 %collective-permute-start.5 = (f32[8,128]{1,0:T(8,128)S(1)}, f32[8,128]{1,0:T(8,128)S(1)}, u32[]{:S(2)}, u32[]{:S(2)}) collective-permute-start(f32[8,128]{1,0:T(8,128)S(1)} %broadcast_add_fusion), channel_id=1, source_target_pairs={{0,2},{1,3},{2,0},{3,1},{4,6},{5,7},{6,4},{7,5},{8,10},{9,11},{10,... | collective-permute-start | bytes 12296 | tf_op jit(solution)/shard_map/ppermute | solution.py:64
  245.4 2.8 copy-start.6
Sparse Core Ops, SparseCore 0:
  31.8 94.4 reduce-scatter.1
  140.3 44.2 all-reduce.4
  213.4 28.1 all-gather.5
  249.3 25.6 all-gather.3

commit v5 on v0

--- a/solution.py
+++ b/solution.py
@@ -133,7 +133,7 @@
         clip * proj_rows, first_moment[layer_index], second_moment[layer_index]
     )
     update_here = jnp.dot(
-        basis_here, lax.all_gather(direction, SHARD, axis=0, tiled=True), precision=exact_mode
+        basis_here, lax.all_gather(direction, SHARD, axis=0, tiled=True), precision=ns_mode
     )
 
     current = refreshed / jnp.sqrt(jnp.sum(refreshed * refreshed) + ns_eps)

time: 282 us -> 280 us (level)
  no operation moved by 1% of the time
where the time goes in v5:
time: 280 us
  waiting for transfers between devices  182 us (65%)
  matrix products  47.6 us (17%)
  between operations  17 us (6%)
  other arithmetic  15.5 us (6%)
  starting transfers between devices  11.8 us (4%)
  local copies, waits for them, and re-layouts  5.64 us (2%)
    reduce_scatter x1, waiting for transfers between devices, shards(): lax.psum_scatter(partial_grad, SHARD, scatter_dimension=0, tiled=True)  94.5 us
    psum x1, waiting for transfers between devices, chip_then_y_sum(): mine = lax.psum(mine, 'chip_y')  44.4 us
    dot_general x1, matrix products, shards(): lax.dot_general(tokens_in, grads_out, (((0,), (0,)), ((), ())), preferred...  24.3 us
    all_gather x1, waiting for transfers between devices, shards(): refreshed = lax.all_gather(packed_r[:rows_here], SHARD, axis=0, tiled=True)  15.6 us
    ppermute x4, waiting for transfers between devices, butterfly_sum(): x = x + lax.ppermute(x, axis, [(i, i ^ k) for i in range(n)])  14.4 us
    dot_general x5, matrix products, mixer_of(): gram = jnp.dot(current.T, current, precision=ns_mode)  9.45 us
    ppermute x4, starting transfers between devices, butterfly_sum(): x = x + lax.ppermute(x, axis, [(i, i ^ k) for i in range(n)])  8.25 us
    all_gather x1, waiting for transfers between devices, shards(): lax.all_gather(direction, SHARD, axis=0, tiled=True)  7.96 us
  transfers between devices with their start and end apart: 10, of which 10 were waited for; matrix products, arithmetic and copies ran while one was open for 8% of the time, Pallas kernels for 0%

profile of v5, /device:TPU:1, one launch (start us, length us, event | category | flops | bytes accessed | tf_op | source)
XLA Modules:
  0.0 279.6 jit_solution(8951538510791465252)
XLA Ops:
  7.2 0.0 copy-start
  7.2 0.0 reduce-scatter.2.cloned.1.call-start
  7.2 24.3 %fusion = f32[2048,2048]{1,0:T(8,128)} fusion(bf16[1,2048,2048]{2,1,0:T(8,128)(2,1)} %param.13, bf16[1,2048,2048]{2,1,0:T(8,128)(2,1)} %param.12), kind=kOutput, calls=%fused_computation | convolution fusion | flops 17179869184 | bytes 33554432 | tf_op jit(solution)/shard_map/dot_general | solution.py:101
  31.6 0.0 reduce-scatter.2.cloned.1.call-update
  31.6 0.0 all-reduce.4.cloned.1.call-start
  31.6 94.5 %reduce-scatter.2.cloned.1.call-done = f32[256,2048]{1,0:T(8,128)} async-done(((f32[2048,2048]{1,0:T(8,128)}), f32[256,2048]{1,0:T(8,128)}) %reduce-scatter.2.cloned.1.call-update) | async-done | bytes 2097168 | tf_op jit(solution)/shard_map/reduce_scatter | solution.py:104
  126.2 2.9 %multiply_reduce_fusion.1 = f32[]{:T(128)} fusion(f32[256,2048]{1,0:T(8,128)} %reduce-scatter.2.cloned.1.call-done), kind=kLoop, calls=%fused_computation.16 | loop fusion | flops 1048575 | bytes 2097156 | tf_op jit(solution)/shard_map/reduce_sum | solution.py:110
  129.1 2.0 convolution_bitcast_fusion.1
  131.1 0.9 select_maximum_fusion
  132.0 1.4 copy-done.4
  133.4 0.1 constant_dynamic-slice_fusion.1
  133.5 1.3 collective-permute-start
  134.8 2.5 collective-permute-done
  137.3 2.7 dynamic-slice_add_fusion
  140.0 0.0 all-reduce.4.cloned.1.call-update
  140.0 0.0 all-gather.5.cloned.1.call-start
  140.1 44.4 %all-reduce.4.cloned.1.call-done = f32[136,2048]{1,0:T(8,128)} async-done(((f32[136,2048]{1,0:T(8,128)}), f32[136,2048]{1,0:T(8,128)}) %all-reduce.4.cloned.1.call-update) | async-done | bytes 1114128 | tf_op jit(solution)/shard_map/psum | solution.py:76
  184.5 2.1 collective-permute-start.1
  186.6 2.7 collective-permute-done.1
  189.3 1.7 broadcast_select_fusion.1
  191.0 0.0 copy-start.2
  191.0 0.5 slice.56
  191.6 1.9 fusion.3
  193.5 0.0 copy-start.6
  193.5 0.7 select_maximum_fusion.1
  194.2 1.4 collective-permute-start.2
  195.6 6.4 %collective-permute-done.2 = f32[264,256]{1,0:T(8,128)S(1)} collective-permute-done((f32[264,256]{1,0:T(8,128)S(1)}, f32[264,256]{1,0:T(8,128)S(1)}, u32[]{:S(2)}, u32[]{:S(2)}) %collective-permute-start.2) | collective-permute-done | bytes 270368 | tf_op jit(solution)/shard_map/ppermute | solution.py:64
  202.0 0.7 fusion.25
  202.6 2.9 %collective-permute-start.3 = (f32[264,256]{1,0:T(8,128)S(1)}, f32[264,256]{1,0:T(8,128)S(1)}, u32[]{:S(2)}, u32[]{:S(2)}) collective-permute-start(f32[264,256]{1,0:T(8,128)S(1)} %fusion.25), channel_id=1, source_target_pairs={{0,8},{4,12},{8,0},{12,4},{1,9},{5,13},{9,1},{13,5},{2,10},{6,14},... | collective-permute-start | bytes 811016 | tf_op jit(solution)/shard_map/ppermute | solution.py:64
  205.6 5.5 %collective-permute-done.3 = f32[264,256]{1,0:T(8,128)S(1)} collective-permute-done((f32[264,256]{1,0:T(8,128)S(1)}, f32[264,256]{1,0:T(8,128)S(1)}, u32[]{:S(2)}, u32[]{:S(2)}) %collective-permute-start.3) | collective-permute-done | bytes 270368 | tf_op jit(solution)/shard_map/ppermute | solution.py:64
  211.1 0.7 slice.59
  211.8 0.0 all-gather.5.cloned.1.call-update
  211.8 0.0 all-gather.3.cloned.1.call-start
  211.9 0.6 fusion.30
  212.5 0.5 slice.57
  214.3 1.3 collective-permute-start.4
  215.6 1.3 collective-permute-done.4
  216.9 2.7 collective-permute-start.5
  219.6 1.3 collective-permute-done.5
  220.8 0.5 slice.54
  222.1 0.8 fusion.17
  222.9 0.9 fusion.16
  223.8 0.0 all-gather.3.cloned.1.call-update
  223.9 0.6 add_divide_fusion.1
  224.5 15.6 %all-gather.5.cloned.1.call-done = f32[2048,256]{1,0:T(8,128)} async-done(((f32[256,256]{1,0:T(8,128)}), f32[2048,256]{1,0:T(8,128)}) %all-gather.5.cloned.1.call-update) | async-done | bytes 2097168 | tf_op jit(solution)/shard_map/all_gather | solution.py:124
  240.0 2.9 %multiply_reduce_fusion = f32[]{:T(128)} fusion(f32[2048,256]{1,0:T(8,128)} %all-gather.5.cloned.1.call-done), kind=kLoop, calls=%fused_computation.15 | loop fusion | flops 1048575 | bytes 2097156 | tf_op jit(solution)/shard_map/reduce_sum | solution.py:139
  243.6 1.8 fusion.27
  245.4 0.3 fusion.8
  245.7 1.0 fusion.26
  246.7 2.0 fusion.10
  248.8 0.3 fusion.7
  249.0 1.2 convolution_add_fusion.2
  250.3 1.9 fusion.31
  252.1 0.3 fusion.6
  252.4 1.1 convolution_add_fusion.1
  253.5 1.9 fusion.32
  255.6 0.3 fusion.5
  255.9 1.0 convolution_add_fusion
  256.9 1.9 fusion.33
  258.8 0.3 fusion.4
  259.1 0.8 fusion.9
  259.9 8.0 %all-gather.3.cloned.1.call-done = f32[256,2048]{1,0:T(8,128)} async-done(((f32[32,2048]{1,0:T(8,128)}), f32[256,2048]{1,0:T(8,128)}) %all-gather.3.cloned.1.call-update) | async-done | bytes 2097168 | tf_op jit(solution)/shard_map/all_gather | solution.py:136
  267.9 3.4 %convolution_bitcast_fusion = f32[1,256,2048]{1,2,0:T(8,128)S(1)} fusion(f32[256,2048]{1,0:T(8,128)} %all-gather.3.cloned.1.call-done, f32[1,256,256]{2,1,0:T(8,128)S(1)} %copy-done), kind=kOutput, calls=%fused_computation.6 | convolution fusion | flops 805306368 | bytes 4456448 | tf_op jit(solution)/shard_map/dot_general | solution.py:135
  271.3 1.8 copy.15
  (22 shorter events, 0.1 us)
Async XLA Ops:
  7.2 121.9 %copy-start = (f32[1,256,256]{2,1,0:T(8,128)S(1)}, f32[1,256,256]{2,1,0:T(8,128)}, u32[]{:S(2)}) copy-start(f32[1,256,256]{2,1,0:T(8,128)} %param.14) | copy-start | bytes 786436
  7.2 119.0 %reduce-scatter.2.cloned.1.call-start = ((), (), s32[]{:S(2)}) async-start(), calls=%async_computation.1 | async-start | bytes 18874368 | tf_op jit(solution)/shard_map/reduce_scatter | solution.py:104
  31.6 152.9 %all-reduce.4.cloned.1.call-start = ((), (), s32[]{:S(2)}) async-start(), calls=%async_computation.2 | async-start | bytes 2228224 | tf_op jit(solution)/shard_map/psum | solution.py:76
  126.2 2.9 %copy-start.1 = (f32[256,2048]{1,0:T(8,128)S(1)}, f32[256,2048]{1,0:T(8,128)}, u32[]{:S(2)}) copy-start(f32[256,2048]{1,0:T(8,128)} %reduce-scatter.2.cloned.1.call-done) | copy-start | bytes 6291460
  129.1 2.0 copy-start.8
  132.0 1.4 copy-start.4
  133.5 3.8 %collective-permute-start = (f32[136,2048]{1,0:T(8,128)S(1)}, f32[136,2048]{1,0:T(8,128)}, u32[]{:S(2)}, u32[]{:S(2)}) collective-permute-start(f32[136,2048]{1,0:T(8,128)S(1)} %constant_dynamic-slice_fusion.1), channel_id=1, source_target_pairs={{0,16},{16,0},{1,17},{17,1},{2,18},{18,2},{3,19},{19,3},{4,20},{20... | collective-permute-start | bytes 3342344 | tf_op jit(solution)/shard_map/ppermute | solution.py:75
  140.0 100.0 %all-gather.5.cloned.1.call-start = ((), (), s32[]{:S(2)}) async-start(), calls=%async_computation.4 | async-start | bytes 2359296 | tf_op jit(solution)/shard_map/all_gather | solution.py:124
  184.5 4.8 %collective-permute-start.1 = (f32[136,2048]{1,0:T(8,128)}, f32[136,2048]{1,0:T(8,128)}, u32[]{:S(2)}, u32[]{:S(2)}) collective-permute-start(f32[136,2048]{1,0:T(8,128)} %all-reduce.4.cloned.1.call-done), channel_id=1, source_target_pairs={{0,16},{16,0},{1,17},{17,1},{2,18},{18,2},{3,19},{19,3},{4,20},{20... | collective-permute-start | bytes 3342344 | tf_op jit(solution)/shard_map/ppermute | solution.py:77
  191.0 2.5 copy-start.2
  193.5 28.6 %copy-start.6 = (f32[1,32,2048]{2,1,0:T(8,128)S(1)}, f32[1,32,2048]{2,1,0:T(8,128)}, u32[]{:S(2)}) copy-start(f32[1,32,2048]{2,1,0:T(8,128)} %param.16) | copy-start | bytes 786436
  194.2 27.9 %copy-start.3 = (f32[136,2048]{1,0:T(8,128)S(1)}, f32[136,2048]{1,0:T(8,128)}, u32[]{:S(2)}) copy-start(f32[136,2048]{1,0:T(8,128)} %copy-done.2) | copy-start | bytes 3342340
  194.2 7.7 %collective-permute-start.2 = (f32[264,256]{1,0:T(8,128)S(1)}, f32[264,256]{1,0:T(8,128)S(1)}, u32[]{:S(2)}, u32[]{:S(2)}) collective-permute-start(f32[264,256]{1,0:T(8,128)S(1)} %select_maximum_fusion.1), channel_id=1, source_target_pairs={{0,4},{4,0},{8,12},{12,8},{1,5},{5,1},{9,13},{13,9},{2,6},{6,2},{1... | collective-permute-start | bytes 811016 | tf_op jit(solution)/shard_map/ppermute | solution.py:64
  202.6 8.4 %collective-permute-start.3 = (f32[264,256]{1,0:T(8,128)S(1)}, f32[264,256]{1,0:T(8,128)S(1)}, u32[]{:S(2)}, u32[]{:S(2)}) collective-permute-start(f32[264,256]{1,0:T(8,128)S(1)} %fusion.25), channel_id=1, source_target_pairs={{0,8},{4,12},{8,0},{12,4},{1,9},{5,13},{9,1},{13,5},{2,10},{6,14},... | collective-permute-start | bytes 811016 | tf_op jit(solution)/shard_map/ppermute | solution.py:64
  211.1 11.8 %copy-start.7 = (f32[1,32,2048]{2,1,0:T(8,128)S(1)}, f32[1,32,2048]{2,1,0:T(8,128)}, u32[]{:S(2)}) copy-start(f32[1,32,2048]{2,1,0:T(8,128)} %param.15) | copy-start | bytes 786436
  211.8 56.0 %all-gather.3.cloned.1.call-start = ((), (), s32[]{:S(2)}) async-start(), calls=%async_computation.3 | async-start | bytes 2359296 | tf_op jit(solution)/shard_map/all_gather | solution.py:136
  214.3 2.5 collective-permute-start.4
  216.9 4.0 %collective-permute-start.5 = (f32[8,128]{1,0:T(8,128)S(1)}, f32[8,128]{1,0:T(8,128)S(1)}, u32[]{:S(2)}, u32[]{:S(2)}) collective-permute-start(f32[8,128]{1,0:T(8,128)S(1)} %broadcast_add_fusion), channel_id=1, source_target_pairs={{0,2},{1,3},{2,0},{3,1},{4,6},{5,7},{6,4},{7,5},{8,10},{9,11},{10,... | collective-permute-start | bytes 12296 | tf_op jit(solution)/shard_map/ppermute | solution.py:64
  222.1 1.8 copy-start.9
  222.1 1.8 copy-start.10
  240.0 3.6 %copy-start.5 = (f32[2048,256]{1,0:T(8,128)S(1)}, f32[2048,256]{1,0:T(8,128)}, u32[]{:S(2)}) copy-start(f32[2048,256]{1,0:T(8,128)} %all-gather.5.cloned.1.call-done) | copy-start | bytes 6291460
Sparse Core Ops, SparseCore 0:
  31.7 94.4 reduce-scatter.1
  140.2 44.2 all-reduce.3
  212.0 28.0 all-gather.4
  242.2 25.6 all-gather.2
